TPU v7x, 256 devices: a whole 4x4x8 slice. The times are simulated.
256 devices in a mesh: seq: 32 (over x, z), tp: 8 (over y, core).
Axes of the slice: x: 4, y: 4, z: 8, core: 2. Of those that a mesh axis runs over, the one named last changes fastest.
Arguments:
- tokens: bfloat16 [32768, 2048], P('seq', 'tp'), may hold values from -6 to 6
- w_inner: bfloat16 [2048, 2, 4096], P('seq', None, 'tp'), may hold values from -0.125 to 0.125
- w_states: bfloat16 [2048, 256], P('seq'), may hold values from -0.125 to 0.125
- w_step: bfloat16 [2048, 64], P('seq', 'tp'), may hold values from -0.125 to 0.125
- conv_inner: float32 [4, 4096], P(None, 'tp'), may hold values from -3 to 3
- conv_states: float32 [4, 256], replicated, may hold values from -3 to 3
- decay_rate: float32 [64], P('tp'), may hold values from 0 to 1, as said below
- step_bias: float32 [64], P('tp'), may hold values from -1 to 0.5
- skip_gain: float32 [64], P('tp'), may hold values from 0.5 to 1.5
- norm_gain: float32 [4096], P('tp'), may hold values from 0.5 to 1.5
- w_output: bfloat16 [4096, 2048], P('tp', 'seq'), may hold values from -0.09375 to 0.09375
- block_owner: int32 [128], replicated, may hold values from 0 to 19, as said below
- lengths: int32 [20], replicated, may hold values from 1 to 16384, as said below
Outputs:
- mixed: bfloat16 [32768, 2048], P('seq', 'tp')
Inputs may be any that keep to these rules, and one draw needn't show every extreme that they name: `block_owner`: each prompt's blocks are consecutive, prompt r has ceil(lengths[r] / 256) of them, and the prompts follow one another in an order drawn afresh; one prompt has 64 blocks and is neither the first nor the last in that order. `lengths`: one prompt has exactly 16384 tokens. `decay_rate`: Positive.
All inputs are finite; a program needn't handle non-finite values.
Results may differ from a plain program's by a relative error of at most 0.0075.
Values may be sent and summed in bfloat16 or wider, within the bound.
No kernel may reach another device: no remote copies, remote signals or barrier semaphores. Data moves between devices by JAX's collectives and lax.ppermute only.
A program may use at most 64 MiB of HBM per device.

v0:
```python
import jax
import jax.numpy as jnp
from jax import lax
from jax.sharding import PartitionSpec as P

BLOCK = 256


def passed_along(value, axis, by):
    count = lax.axis_size(axis)
    pairs = [(i, i + by) for i in range(count) if 0 <= i + by < count]
    return lax.ppermute(value, axis, pairs)


def convolve(values, edge_rows, weights, in_block, carry_on):
    lag_rows = weights.shape[0] - 1
    row_total = values.shape[0]
    widened = jnp.concatenate([edge_rows, values], axis=0).astype(jnp.float32)
    total = jnp.zeros(values.shape, jnp.float32)
    for offset in range(weights.shape[0]):
        shifted = widened[lag_rows - offset : lag_rows - offset + row_total]
        keeping = (in_block >= offset) | carry_on
        total = total + jnp.where(keeping[:, None], shifted, 0.0) * weights[offset]
    return jax.nn.silu(total).astype(jnp.bfloat16)


def on_device(
    tokens,
    w_inner,
    w_states,
    w_step,
    conv_inner,
    conv_states,
    decay_rate,
    step_bias,
    skip_gain,
    norm_gain,
    w_output,
    block_owner,
    lengths,
):
    row_count = tokens.shape[0]
    local_blocks = row_count // BLOCK
    total_blocks = block_owner.shape[0]
    heads_here = w_step.shape[1]
    inner_here = w_inner.shape[2]
    state_size = w_states.shape[1] // 2
    head_size = inner_here // heads_here
    lag_rows = conv_inner.shape[0] - 1
    block_ids = jnp.arange(total_blocks, dtype=jnp.int32)
    same_owner = block_owner[:, None] == block_owner[None, :]
    first_block = jnp.min(jnp.where(same_owner, block_ids[None, :], total_blocks), axis=1)
    starting = (first_block == block_ids).astype(jnp.int32)
    request_ids = jnp.arange(lengths.shape[0], dtype=jnp.int32)
    own_length = jnp.sum(
        jnp.where(block_owner[:, None] == request_ids[None, :], lengths[None, :], 0), axis=1
    )
    valid_rows = jnp.clip(own_length - (block_ids - first_block) * BLOCK, 0, BLOCK)
    seq_index = lax.axis_index("seq")
    local_start = lax.dynamic_slice_in_dim(starting, seq_index * local_blocks, local_blocks)
    local_valid = lax.dynamic_slice_in_dim(valid_rows, seq_index * local_blocks, local_blocks)
    in_block = jnp.arange(row_count, dtype=jnp.int32) % BLOCK
    carry_on = jnp.repeat(local_start == 0, BLOCK)
    whole = lax.all_gather(tokens, "tp", axis=1, tiled=True)
    pieces = (
        lax.all_gather(w_inner, "seq", axis=0, tiled=True),
        lax.all_gather(w_states, "seq", axis=0, tiled=True),
        lax.all_gather(w_step, "seq", axis=0, tiled=True),
    )
    count = pieces[0].shape[0]
    inner_sum = jnp.dot(
        whole, pieces[0].reshape(count, 2 * inner_here), preferred_element_type=jnp.float32
    )
    states_sum = jnp.dot(whole, pieces[1], preferred_element_type=jnp.float32)
    step_sum = jnp.dot(whole, pieces[2], preferred_element_type=jnp.float32)
    projected = inner_sum.astype(jnp.bfloat16)
    gate_in = projected[:, :inner_here]
    x_in = projected[:, inner_here:]
    bc_in = states_sum.astype(jnp.bfloat16)
    step_raw = step_sum.astype(jnp.bfloat16)
    edge_inner, edge_states = passed_along(
        (x_in[row_count - lag_rows :], bc_in[row_count - lag_rows :]), "seq", 1
    )
    x_conv = convolve(x_in, edge_inner, conv_inner, in_block, carry_on)
    bc_conv = convolve(bc_in, edge_states, conv_states, in_block, carry_on)
    step_size = jax.nn.softplus(step_raw.astype(jnp.float32) + step_bias)
    log_decay = -decay_rate * step_size
    x_heads = x_conv.reshape(local_blocks, BLOCK, heads_here, head_size)
    b_rows = bc_conv[:, :state_size].reshape(local_blocks, BLOCK, state_size)
    c_rows = bc_conv[:, state_size:].reshape(local_blocks, BLOCK, state_size)
    step_blocks = step_size.reshape(local_blocks, BLOCK, heads_here)
    cumulative = jnp.cumsum(log_decay.reshape(local_blocks, BLOCK, heads_here), axis=1)
    causal = jnp.arange(BLOCK)[:, None] >= jnp.arange(BLOCK)[None, :]
    spread = cumulative[:, :, None, :] - cumulative[:, None, :, :]
    decays = jnp.exp(jnp.where(causal[None, :, :, None], spread, -jnp.inf))
    intersection = jnp.einsum("cin,cjn->cij", c_rows, b_rows, preferred_element_type=jnp.float32)
    mixing = (decays * intersection[:, :, :, None] * step_blocks[:, None, :, :]).astype(
        jnp.bfloat16
    )
    y_inner = jnp.einsum("cijh,cjhp->cihp", mixing, x_heads, preferred_element_type=jnp.float32)
    final_log = cumulative[:, -1, :]
    tail_weight = jnp.exp(final_log[:, None, :] - cumulative) * step_blocks
    weighted_b = (tail_weight[:, :, :, None] * b_rows.astype(jnp.float32)[:, :, None, :]).astype(
        jnp.bfloat16
    )
    fresh = jnp.einsum("cjhn,cjhp->chnp", weighted_b, x_heads, preferred_element_type=jnp.float32)
    keep_flag = jnp.where(local_start == 1, 0.0, 1.0).astype(jnp.float32)
    block_gain_each = jnp.exp(final_log) * keep_flag[:, None]

    def fold_block(carry, item):
        gain_now, fresh_now = item
        return ((carry[0] * gain_now, gain_now[:, None, None] * carry[1] + fresh_now), None)

    zero_state = jnp.zeros((heads_here, state_size, head_size), jnp.float32)
    unit_gain = jnp.ones((heads_here,), jnp.float32)
    (block_gain, block_state), _ = lax.scan(
        fold_block, (unit_gain, zero_state), (block_gain_each, fresh)
    )

    def relay(iteration, entering_now):
        return passed_along(block_gain[:, None, None] * entering_now + block_state, "seq", 1)

    entering = lax.fori_loop(0, lax.axis_size("seq") - 1, relay, zero_state)

    def pass_block(previous, item):
        log_now, keep_now, fresh_now = item
        incoming = previous * keep_now
        return (jnp.exp(log_now)[:, None, None] * incoming + fresh_now, incoming)

    _, incoming_all = lax.scan(pass_block, entering, (final_log, keep_flag, fresh))
    incoming_half = incoming_all.astype(jnp.bfloat16)
    y_carry = jnp.exp(cumulative)[:, :, :, None] * jnp.einsum(
        "cin,chnp->cihp", c_rows, incoming_half, preferred_element_type=jnp.float32
    )
    y_total = (y_inner + y_carry).reshape(row_count, inner_here) + jnp.repeat(skip_gain, head_size)[
        None, :
    ] * x_conv.astype(jnp.float32)
    gated = y_total * jax.nn.silu(gate_in.astype(jnp.float32))
    squares = lax.psum(jnp.sum(gated * gated, axis=1), "tp")
    square_mean = squares / (inner_here * lax.axis_size("tp"))
    normed = (gated * lax.rsqrt(square_mean + 1e-05)[:, None] * norm_gain).astype(jnp.bfloat16)
    partial_out = jnp.dot(
        normed,
        lax.all_gather(w_output, "seq", axis=1, tiled=True),
        preferred_element_type=jnp.float32,
    )
    summed = lax.psum_scatter(partial_out, "tp", scatter_dimension=1, tiled=True)
    live = in_block < jnp.repeat(local_valid, BLOCK)
    return jnp.where(live[:, None], summed, 0.0).astype(jnp.bfloat16)


def solution(mesh):
    return jax.shard_map(
        on_device,
        mesh=mesh,
        in_specs=(
            P("seq", "tp"),
            P("seq", None, "tp"),
            P("seq", None),
            P("seq", "tp"),
            P(None, "tp"),
            P(),
            P("tp"),
            P("tp"),
            P("tp"),
            P("tp"),
            P("tp", "seq"),
            P(),
            P(),
        ),
        out_specs=P("seq", "tp"),
        check_vma=False,
    )
```

profile of v0, /device:TPU:1, one launch (start us, length us, event | category | flops | bytes accessed | tf_op | source)
XLA Modules:
  0.0 875.8 jit_solution(9368195072958447139)
XLA Ops:
  13.4 41.9 %all-gather = bf16[32,64,8]{1,2,0:T(8,128)(2,1)S(1)} all-gather(bf16[1,64,8]{1,2,0:T(8,128)(2,1)} %bitcast.99), channel_id=1, replica_groups=mesh['seq'=32,'tp'=8] {'seq'}, dimensions={0}, use_global_device_ids=true | all-gather | bytes 33792 | tf_op jit(solution)/shard_map/all_gather | solution.py:68
  57.5 27.5 %all-gather.10.cloned.1.call-done = bf16[2048,256]{1,0:T(8,128)(2,1)} async-done(((bf16[64,256]{1,0:T(8,128)(2,1)}), bf16[2048,256]{1,0:T(8,128)(2,1)}) %all-gather.10.cloned.1.call-update) | async-done | bytes 1048592 | tf_op jit(solution)/shard_map/all_gather | solution.py:67
  85.0 42.9 %all-gather.6.cloned.1.call-done = bf16[1024,2048]{1,0:T(8,128)(2,1)} async-done(((bf16[1024,256]{1,0:T(8,128)(2,1)}), bf16[1024,2048]{1,0:T(8,128)(2,1)}) %all-gather.6.cloned.1.call-update) | async-done | bytes 4194320 | tf_op jit(solution)/shard_map/all_gather | solution.py:64
  141.9 67.3 %all-gather.8.cloned.1.call-done = bf16[2048,2,512]{2,1,0:T(2,128)(2,1)} async-done(((bf16[64,2,512]{2,1,0:T(2,128)(2,1)}), bf16[2048,2,512]{2,1,0:T(2,128)(2,1)}) %all-gather.8.cloned.1.call-update) | async-done | bytes 4194320 | tf_op jit(solution)/shard_map/all_gather | solution.py:66
  212.8 4.7 convolution_convert_fusion
  233.1 5.1 fusion.14
  238.2 7.3 while.37
  245.5 454.9 %while.35 = (s32[]{:T(128)}, f32[8,128,64]{2,1,0:T(8,128)S(1)}, f32[8]{0:T(128)S(1)}, f32[8,128,64]{2,1,0:T(8,128)S(1)}, s32[]{:T(128)}) while((s32[]{:T(128)}, f32[8,128,64]{2,1,0:T(8,128)S(1)}, f32[8]{0:T(128)S(1)}, f32[8,128,64]{2,1,0:T(8,128)S(1)}, s32[]{:T(128)}) %tuple.77), condition=%wide.region_7.8_spmd, body=%wide.region_6.7_spmd.sunk | while | flops 131074 | bytes 1835141 | solution.py:123
  249.8 7.4 collective-permute-done
  262.2 9.9 %collective-permute-done = f32[8,128,64]{2,1,0:T(8,128)S(1)} collective-permute-done((f32[8,128,64]{2,1,0:T(8,128)}, f32[8,128,64]{2,1,0:T(8,128)S(1)}, u32[]{:S(2)}, u32[]{:S(2)}) %collective-permute-start) | collective-permute-done | bytes 262176 | tf_op jit(solution)/shard_map/while/body/eval_jaxpr/ppermute | solution.py:12
  277.4 11.2 %collective-permute-done = f32[8,128,64]{2,1,0:T(8,128)S(1)} collective-permute-done((f32[8,128,64]{2,1,0:T(8,128)}, f32[8,128,64]{2,1,0:T(8,128)S(1)}, u32[]{:S(2)}, u32[]{:S(2)}) %collective-permute-start) | collective-permute-done | bytes 262176 | tf_op jit(solution)/shard_map/while/body/eval_jaxpr/ppermute | solution.py:12
  293.7 6.4 collective-permute-done
  304.7 7.2 collective-permute-done
  316.6 8.4 collective-permute-done
  329.6 9.5 %collective-permute-done = f32[8,128,64]{2,1,0:T(8,128)S(1)} collective-permute-done((f32[8,128,64]{2,1,0:T(8,128)}, f32[8,128,64]{2,1,0:T(8,128)S(1)}, u32[]{:S(2)}, u32[]{:S(2)}) %collective-permute-start) | collective-permute-done | bytes 262176 | tf_op jit(solution)/shard_map/while/body/eval_jaxpr/ppermute | solution.py:12
  343.8 10.7 %collective-permute-done = f32[8,128,64]{2,1,0:T(8,128)S(1)} collective-permute-done((f32[8,128,64]{2,1,0:T(8,128)}, f32[8,128,64]{2,1,0:T(8,128)S(1)}, u32[]{:S(2)}, u32[]{:S(2)}) %collective-permute-start) | collective-permute-done | bytes 262176 | tf_op jit(solution)/shard_map/while/body/eval_jaxpr/ppermute | solution.py:12
  359.2 11.8 %collective-permute-done = f32[8,128,64]{2,1,0:T(8,128)S(1)} collective-permute-done((f32[8,128,64]{2,1,0:T(8,128)}, f32[8,128,64]{2,1,0:T(8,128)S(1)}, u32[]{:S(2)}, u32[]{:S(2)}) %collective-permute-start) | collective-permute-done | bytes 262176 | tf_op jit(solution)/shard_map/while/body/eval_jaxpr/ppermute | solution.py:12
  371.9 4.8 collective-permute-start
  376.7 12.0 %collective-permute-done = f32[8,128,64]{2,1,0:T(8,128)S(1)} collective-permute-done((f32[8,128,64]{2,1,0:T(8,128)}, f32[8,128,64]{2,1,0:T(8,128)S(1)}, u32[]{:S(2)}, u32[]{:S(2)}) %collective-permute-start) | collective-permute-done | bytes 262176 | tf_op jit(solution)/shard_map/while/body/eval_jaxpr/ppermute | solution.py:12
  389.6 5.3 collective-permute-start
  394.9 10.9 %collective-permute-done = f32[8,128,64]{2,1,0:T(8,128)S(1)} collective-permute-done((f32[8,128,64]{2,1,0:T(8,128)}, f32[8,128,64]{2,1,0:T(8,128)S(1)}, u32[]{:S(2)}, u32[]{:S(2)}) %collective-permute-start) | collective-permute-done | bytes 262176 | tf_op jit(solution)/shard_map/while/body/eval_jaxpr/ppermute | solution.py:12
  411.4 9.8 %collective-permute-done = f32[8,128,64]{2,1,0:T(8,128)S(1)} collective-permute-done((f32[8,128,64]{2,1,0:T(8,128)}, f32[8,128,64]{2,1,0:T(8,128)S(1)}, u32[]{:S(2)}, u32[]{:S(2)}) %collective-permute-start) | collective-permute-done | bytes 262176 | tf_op jit(solution)/shard_map/while/body/eval_jaxpr/ppermute | solution.py:12
  426.1 8.6 collective-permute-done
  435.7 5.2 collective-permute-start
  440.9 7.8 collective-permute-done
  449.6 5.2 collective-permute-start
  454.8 6.9 collective-permute-done
  462.7 5.2 collective-permute-start
  467.9 6.4 collective-permute-done
  475.2 5.2 collective-permute-start
  480.4 6.4 collective-permute-done
  487.7 5.2 collective-permute-start
  493.0 6.4 collective-permute-done
  500.3 5.2 collective-permute-start
  505.5 7.1 collective-permute-done
  513.5 5.4 collective-permute-start
  519.0 8.3 collective-permute-done
  528.1 4.8 collective-permute-start
  533.0 8.7 collective-permute-done
  542.5 6.1 collective-permute-start
  548.7 9.5 %collective-permute-done = f32[8,128,64]{2,1,0:T(8,128)S(1)} collective-permute-done((f32[8,128,64]{2,1,0:T(8,128)}, f32[8,128,64]{2,1,0:T(8,128)S(1)}, u32[]{:S(2)}, u32[]{:S(2)}) %collective-permute-start) | collective-permute-done | bytes 262176 | tf_op jit(solution)/shard_map/while/body/eval_jaxpr/ppermute | solution.py:12
  559.1 7.0 collective-permute-start
  566.1 10.6 %collective-permute-done = f32[8,128,64]{2,1,0:T(8,128)S(1)} collective-permute-done((f32[8,128,64]{2,1,0:T(8,128)}, f32[8,128,64]{2,1,0:T(8,128)S(1)}, u32[]{:S(2)}, u32[]{:S(2)}) %collective-permute-start) | collective-permute-done | bytes 262176 | tf_op jit(solution)/shard_map/while/body/eval_jaxpr/ppermute | solution.py:12
  577.7 7.6 collective-permute-start
  585.3 11.8 %collective-permute-done = f32[8,128,64]{2,1,0:T(8,128)S(1)} collective-permute-done((f32[8,128,64]{2,1,0:T(8,128)}, f32[8,128,64]{2,1,0:T(8,128)S(1)}, u32[]{:S(2)}, u32[]{:S(2)}) %collective-permute-start) | collective-permute-done | bytes 262176 | tf_op jit(solution)/shard_map/while/body/eval_jaxpr/ppermute | solution.py:12
  598.0 7.7 collective-permute-start
  605.7 11.1 %collective-permute-done = f32[8,128,64]{2,1,0:T(8,128)S(1)} collective-permute-done((f32[8,128,64]{2,1,0:T(8,128)}, f32[8,128,64]{2,1,0:T(8,128)S(1)}, u32[]{:S(2)}, u32[]{:S(2)}) %collective-permute-start) | collective-permute-done | bytes 262176 | tf_op jit(solution)/shard_map/while/body/eval_jaxpr/ppermute | solution.py:12
  617.7 6.7 collective-permute-start
  624.5 9.9 %collective-permute-done = f32[8,128,64]{2,1,0:T(8,128)S(1)} collective-permute-done((f32[8,128,64]{2,1,0:T(8,128)}, f32[8,128,64]{2,1,0:T(8,128)S(1)}, u32[]{:S(2)}, u32[]{:S(2)}) %collective-permute-start) | collective-permute-done | bytes 262176 | tf_op jit(solution)/shard_map/while/body/eval_jaxpr/ppermute | solution.py:12
  635.3 6.1 collective-permute-start
  641.4 8.8 %collective-permute-done = f32[8,128,64]{2,1,0:T(8,128)S(1)} collective-permute-done((f32[8,128,64]{2,1,0:T(8,128)}, f32[8,128,64]{2,1,0:T(8,128)S(1)}, u32[]{:S(2)}, u32[]{:S(2)}) %collective-permute-start) | collective-permute-done | bytes 262176 | tf_op jit(solution)/shard_map/while/body/eval_jaxpr/ppermute | solution.py:12
  651.1 5.3 collective-permute-start
  656.4 7.6 collective-permute-done
  669.3 6.4 collective-permute-done
  676.6 5.2 collective-permute-start
  681.8 6.4 collective-permute-done
  689.1 5.0 collective-permute-start
  694.1 6.4 collective-permute-done
  700.5 15.3 %while.36 = (s32[]{:T(128)}, f32[8,128,64]{2,1,0:T(8,128)S(1)}, bf16[4,8,128,64]{3,2,1,0:T(8,128)(2,1)}, f32[4,8]{1,0:T(4,128)S(1)}, f32[4]{0:T(128)S(1)}, /*index=5*/f32[4,8,128,64]{3,2,1,0:T(8,128)}, s32[]{:T(128)}) while((s32[]{:T(128)}, f32[8,128,64]{2,1,0:T(8,128)S(1)}, bf16[4,8,128,64]{3,2,1,0:T(8,128)(2,1)}, f32[4,8]{1,0:T(4,128)S(1)}, ...), condition=%wide.region_9.10_spmd, body=%wide.region_8.9_spmd.sunk | while | flops 262146 | bytes 1574085 | solution.py:130
  726.7 4.8 reshape.137
  731.5 5.6 multiply_reduce_fusion
  737.1 48.3 %psum.7 = f32[1024]{0:T(1024)S(1)} all-reduce(f32[1024]{0:T(1024)S(1)} %get-tuple-element.196), channel_id=1, replica_groups=mesh['seq'=32,'tp'=8] {'tp'}, use_global_device_ids=true, to_apply=%region_11.12 | all-reduce | flops 1024 | bytes 8192 | tf_op jit(solution)/shard_map/psum | solution.py:139
  785.4 7.9 fusion.26
  794.3 72.8 %reduce-scatter.2.cloned.1.call-done = f32[1024,256]{1,0:T(8,128)} async-done(((f32[1024,2048]{1,0:T(8,128)}), f32[1024,256]{1,0:T(8,128)}) %reduce-scatter.2.cloned.1.call-update) | async-done | bytes 1048592 | tf_op jit(solution)/shard_map/reduce_scatter | solution.py:147
  (180 shorter events, 154.2 us)
Async XLA Ops:
  6.5 78.4 %all-gather.10.cloned.1.call-start = ((), (), s32[]{:S(2)}) async-start(), calls=%async_computation.3 | async-start | bytes 1081344 | tf_op jit(solution)/shard_map/all_gather | solution.py:67
  7.3 120.7 %all-gather.6.cloned.1.call-start = ((), (), s32[]{:S(2)}) async-start(), calls=%async_computation.1 | async-start | bytes 4718592 | tf_op jit(solution)/shard_map/all_gather | solution.py:64
  8.0 201.3 %all-gather.8.cloned.1.call-start = ((), (), s32[]{:S(2)}) async-start(), calls=%async_computation.2 | async-start | bytes 4325376 | tf_op jit(solution)/shard_map/all_gather | solution.py:66
  8.7 776.7 %all-gather.12.cloned.1.call-start = ((), (), s32[]{:S(2)}) async-start(), calls=%async_computation.4 | async-start | bytes 2162688 | tf_op jit(solution)/shard_map/all_gather | solution.py:144
  9.3 857.7 %reduce-scatter.2.cloned.1.call-start = ((), (), s32[]{:S(2)}) async-start(), calls=%async_computation.5 | async-start | bytes 9437184 | tf_op jit(solution)/shard_map/reduce_scatter | solution.py:147
  10.3 0.5 copy-start.19
  11.0 128.7 %copy-start.15 = (f32[4]{0:T(128)}, f32[4]{0:T(128)S(1)}, u32[]{:S(2)}) copy-start(f32[4]{0:T(128)S(1)} %compare_select_fusion.1) | copy-start | bytes 52
  11.7 211.3 %copy-start.8 = (pred[1024]{0:T(1024)(128)(4,1)}, pred[1024]{0:T(1024)(128)(4,1)S(1)}, u32[]{:S(2)}) copy-start(pred[1024]{0:T(1024)(128)(4,1)S(1)} %get-tuple-element.212) | copy-start | bytes 3076
  11.7 211.3 %copy-start.10 = (pred[1024]{0:T(1024)(128)(4,1)}, pred[1024]{0:T(1024)(128)(4,1)S(1)}, u32[]{:S(2)}) copy-start(pred[1024]{0:T(1024)(128)(4,1)S(1)} %get-tuple-element.213) | copy-start | bytes 3076
  57.5 77.5 %copy-start.14 = (f32[8]{0:T(128)S(1)}, f32[8]{0:T(128)}, u32[]{:S(2)}) copy-start(f32[8]{0:T(128)} %param.26) | copy-start | bytes 100
  127.9 7.1 copy-start
  131.8 8.5 collective-permute-start.2
  209.3 3.5 copy-start.1
  217.5 5.1 copy-start.3
  217.6 5.1 collective-permute-start.1
  230.0 3.1 copy-start.4
  245.5 454.9 %copy-start.16 = (f32[4]{0:T(128)S(1)}, f32[4]{0:T(128)}, u32[]{:S(2)}) copy-start(f32[4]{0:T(128)} %copy-done.15) | copy-start | bytes 52
  246.4 10.8 %collective-permute-start = (f32[8,128,64]{2,1,0:T(8,128)}, f32[8,128,64]{2,1,0:T(8,128)S(1)}, u32[]{:S(2)}, u32[]{:S(2)}) collective-permute-start(f32[8,128,64]{2,1,0:T(8,128)} %multiply_add_fusion.2), channel_id=1, source_target_pairs={{0,8},{8,16},{16,24},{24,32},{32,40},{40,48},{48,56},{56,64},{64,7... | collective-permute-start | bytes 786440 | tf_op jit(solution)/shard_map/while/body/eval_jaxpr/ppermute | solution.py:12
  258.1 14.0 %collective-permute-start = (f32[8,128,64]{2,1,0:T(8,128)}, f32[8,128,64]{2,1,0:T(8,128)S(1)}, u32[]{:S(2)}, u32[]{:S(2)}) collective-permute-start(f32[8,128,64]{2,1,0:T(8,128)} %multiply_add_fusion.2), channel_id=1, source_target_pairs={{0,8},{8,16},{16,24},{24,32},{32,40},{40,48},{48,56},{56,64},{64,7... | collective-permute-start | bytes 786440 | tf_op jit(solution)/shard_map/while/body/eval_jaxpr/ppermute | solution.py:12
  273.0 15.6 %collective-permute-start = (f32[8,128,64]{2,1,0:T(8,128)}, f32[8,128,64]{2,1,0:T(8,128)S(1)}, u32[]{:S(2)}, u32[]{:S(2)}) collective-permute-start(f32[8,128,64]{2,1,0:T(8,128)} %multiply_add_fusion.2), channel_id=1, source_target_pairs={{0,8},{8,16},{16,24},{24,32},{32,40},{40,48},{48,56},{56,64},{64,7... | collective-permute-start | bytes 786440 | tf_op jit(solution)/shard_map/while/body/eval_jaxpr/ppermute | solution.py:12
  289.5 10.5 %collective-permute-start = (f32[8,128,64]{2,1,0:T(8,128)}, f32[8,128,64]{2,1,0:T(8,128)S(1)}, u32[]{:S(2)}, u32[]{:S(2)}) collective-permute-start(f32[8,128,64]{2,1,0:T(8,128)} %multiply_add_fusion.2), channel_id=1, source_target_pairs={{0,8},{8,16},{16,24},{24,32},{32,40},{40,48},{48,56},{56,64},{64,7... | collective-permute-start | bytes 786440 | tf_op jit(solution)/shard_map/while/body/eval_jaxpr/ppermute | solution.py:12
  301.0 11.0 %collective-permute-start = (f32[8,128,64]{2,1,0:T(8,128)}, f32[8,128,64]{2,1,0:T(8,128)S(1)}, u32[]{:S(2)}, u32[]{:S(2)}) collective-permute-start(f32[8,128,64]{2,1,0:T(8,128)} %multiply_add_fusion.2), channel_id=1, source_target_pairs={{0,8},{8,16},{16,24},{24,32},{32,40},{40,48},{48,56},{56,64},{64,7... | collective-permute-start | bytes 786440 | tf_op jit(solution)/shard_map/while/body/eval_jaxpr/ppermute | solution.py:12
  312.9 12.1 %collective-permute-start = (f32[8,128,64]{2,1,0:T(8,128)}, f32[8,128,64]{2,1,0:T(8,128)S(1)}, u32[]{:S(2)}, u32[]{:S(2)}) collective-permute-start(f32[8,128,64]{2,1,0:T(8,128)} %multiply_add_fusion.2), channel_id=1, source_target_pairs={{0,8},{8,16},{16,24},{24,32},{32,40},{40,48},{48,56},{56,64},{64,7... | collective-permute-start | bytes 786440 | tf_op jit(solution)/shard_map/while/body/eval_jaxpr/ppermute | solution.py:12
  325.9 13.3 %collective-permute-start = (f32[8,128,64]{2,1,0:T(8,128)}, f32[8,128,64]{2,1,0:T(8,128)S(1)}, u32[]{:S(2)}, u32[]{:S(2)}) collective-permute-start(f32[8,128,64]{2,1,0:T(8,128)} %multiply_add_fusion.2), channel_id=1, source_target_pairs={{0,8},{8,16},{16,24},{24,32},{32,40},{40,48},{48,56},{56,64},{64,7... | collective-permute-start | bytes 786440 | tf_op jit(solution)/shard_map/while/body/eval_jaxpr/ppermute | solution.py:12
  340.1 14.4 %collective-permute-start = (f32[8,128,64]{2,1,0:T(8,128)}, f32[8,128,64]{2,1,0:T(8,128)S(1)}, u32[]{:S(2)}, u32[]{:S(2)}) collective-permute-start(f32[8,128,64]{2,1,0:T(8,128)} %multiply_add_fusion.2), channel_id=1, source_target_pairs={{0,8},{8,16},{16,24},{24,32},{32,40},{40,48},{48,56},{56,64},{64,7... | collective-permute-start | bytes 786440 | tf_op jit(solution)/shard_map/while/body/eval_jaxpr/ppermute | solution.py:12
  355.4 15.6 %collective-permute-start = (f32[8,128,64]{2,1,0:T(8,128)}, f32[8,128,64]{2,1,0:T(8,128)S(1)}, u32[]{:S(2)}, u32[]{:S(2)}) collective-permute-start(f32[8,128,64]{2,1,0:T(8,128)} %multiply_add_fusion.2), channel_id=1, source_target_pairs={{0,8},{8,16},{16,24},{24,32},{32,40},{40,48},{48,56},{56,64},{64,7... | collective-permute-start | bytes 786440 | tf_op jit(solution)/shard_map/while/body/eval_jaxpr/ppermute | solution.py:12
  371.9 16.8 %collective-permute-start = (f32[8,128,64]{2,1,0:T(8,128)}, f32[8,128,64]{2,1,0:T(8,128)S(1)}, u32[]{:S(2)}, u32[]{:S(2)}) collective-permute-start(f32[8,128,64]{2,1,0:T(8,128)} %multiply_add_fusion.2), channel_id=1, source_target_pairs={{0,8},{8,16},{16,24},{24,32},{32,40},{40,48},{48,56},{56,64},{64,7... | collective-permute-start | bytes 786440 | tf_op jit(solution)/shard_map/while/body/eval_jaxpr/ppermute | solution.py:12
  389.6 16.3 %collective-permute-start = (f32[8,128,64]{2,1,0:T(8,128)}, f32[8,128,64]{2,1,0:T(8,128)S(1)}, u32[]{:S(2)}, u32[]{:S(2)}) collective-permute-start(f32[8,128,64]{2,1,0:T(8,128)} %multiply_add_fusion.2), channel_id=1, source_target_pairs={{0,8},{8,16},{16,24},{24,32},{32,40},{40,48},{48,56},{56,64},{64,7... | collective-permute-start | bytes 786440 | tf_op jit(solution)/shard_map/while/body/eval_jaxpr/ppermute | solution.py:12
  406.7 14.4 %collective-permute-start = (f32[8,128,64]{2,1,0:T(8,128)}, f32[8,128,64]{2,1,0:T(8,128)S(1)}, u32[]{:S(2)}, u32[]{:S(2)}) collective-permute-start(f32[8,128,64]{2,1,0:T(8,128)} %multiply_add_fusion.2), channel_id=1, source_target_pairs={{0,8},{8,16},{16,24},{24,32},{32,40},{40,48},{48,56},{56,64},{64,7... | collective-permute-start | bytes 786440 | tf_op jit(solution)/shard_map/while/body/eval_jaxpr/ppermute | solution.py:12
  422.1 12.7 %collective-permute-start = (f32[8,128,64]{2,1,0:T(8,128)}, f32[8,128,64]{2,1,0:T(8,128)S(1)}, u32[]{:S(2)}, u32[]{:S(2)}) collective-permute-start(f32[8,128,64]{2,1,0:T(8,128)} %multiply_add_fusion.2), channel_id=1, source_target_pairs={{0,8},{8,16},{16,24},{24,32},{32,40},{40,48},{48,56},{56,64},{64,7... | collective-permute-start | bytes 786440 | tf_op jit(solution)/shard_map/while/body/eval_jaxpr/ppermute | solution.py:12
  435.7 13.0 %collective-permute-start = (f32[8,128,64]{2,1,0:T(8,128)}, f32[8,128,64]{2,1,0:T(8,128)S(1)}, u32[]{:S(2)}, u32[]{:S(2)}) collective-permute-start(f32[8,128,64]{2,1,0:T(8,128)} %multiply_add_fusion.2), channel_id=1, source_target_pairs={{0,8},{8,16},{16,24},{24,32},{32,40},{40,48},{48,56},{56,64},{64,7... | collective-permute-start | bytes 786440 | tf_op jit(solution)/shard_map/while/body/eval_jaxpr/ppermute | solution.py:12
  449.6 12.2 %collective-permute-start = (f32[8,128,64]{2,1,0:T(8,128)}, f32[8,128,64]{2,1,0:T(8,128)S(1)}, u32[]{:S(2)}, u32[]{:S(2)}) collective-permute-start(f32[8,128,64]{2,1,0:T(8,128)} %multiply_add_fusion.2), channel_id=1, source_target_pairs={{0,8},{8,16},{16,24},{24,32},{32,40},{40,48},{48,56},{56,64},{64,7... | collective-permute-start | bytes 786440 | tf_op jit(solution)/shard_map/while/body/eval_jaxpr/ppermute | solution.py:12
  462.7 11.6 %collective-permute-start = (f32[8,128,64]{2,1,0:T(8,128)}, f32[8,128,64]{2,1,0:T(8,128)S(1)}, u32[]{:S(2)}, u32[]{:S(2)}) collective-permute-start(f32[8,128,64]{2,1,0:T(8,128)} %multiply_add_fusion.2), channel_id=1, source_target_pairs={{0,8},{8,16},{16,24},{24,32},{32,40},{40,48},{48,56},{56,64},{64,7... | collective-permute-start | bytes 786440 | tf_op jit(solution)/shard_map/while/body/eval_jaxpr/ppermute | solution.py:12
  475.2 11.6 %collective-permute-start = (f32[8,128,64]{2,1,0:T(8,128)}, f32[8,128,64]{2,1,0:T(8,128)S(1)}, u32[]{:S(2)}, u32[]{:S(2)}) collective-permute-start(f32[8,128,64]{2,1,0:T(8,128)} %multiply_add_fusion.2), channel_id=1, source_target_pairs={{0,8},{8,16},{16,24},{24,32},{32,40},{40,48},{48,56},{56,64},{64,7... | collective-permute-start | bytes 786440 | tf_op jit(solution)/shard_map/while/body/eval_jaxpr/ppermute | solution.py:12
  487.7 11.6 %collective-permute-start = (f32[8,128,64]{2,1,0:T(8,128)}, f32[8,128,64]{2,1,0:T(8,128)S(1)}, u32[]{:S(2)}, u32[]{:S(2)}) collective-permute-start(f32[8,128,64]{2,1,0:T(8,128)} %multiply_add_fusion.2), channel_id=1, source_target_pairs={{0,8},{8,16},{16,24},{24,32},{32,40},{40,48},{48,56},{56,64},{64,7... | collective-permute-start | bytes 786440 | tf_op jit(solution)/shard_map/while/body/eval_jaxpr/ppermute | solution.py:12
  500.3 12.4 %collective-permute-start = (f32[8,128,64]{2,1,0:T(8,128)}, f32[8,128,64]{2,1,0:T(8,128)S(1)}, u32[]{:S(2)}, u32[]{:S(2)}) collective-permute-start(f32[8,128,64]{2,1,0:T(8,128)} %multiply_add_fusion.2), channel_id=1, source_target_pairs={{0,8},{8,16},{16,24},{24,32},{32,40},{40,48},{48,56},{56,64},{64,7... | collective-permute-start | bytes 786440 | tf_op jit(solution)/shard_map/while/body/eval_jaxpr/ppermute | solution.py:12
  513.5 13.7 %collective-permute-start = (f32[8,128,64]{2,1,0:T(8,128)}, f32[8,128,64]{2,1,0:T(8,128)S(1)}, u32[]{:S(2)}, u32[]{:S(2)}) collective-permute-start(f32[8,128,64]{2,1,0:T(8,128)} %multiply_add_fusion.2), channel_id=1, source_target_pairs={{0,8},{8,16},{16,24},{24,32},{32,40},{40,48},{48,56},{56,64},{64,7... | collective-permute-start | bytes 786440 | tf_op jit(solution)/shard_map/while/body/eval_jaxpr/ppermute | solution.py:12
  528.1 13.5 %collective-permute-start = (f32[8,128,64]{2,1,0:T(8,128)}, f32[8,128,64]{2,1,0:T(8,128)S(1)}, u32[]{:S(2)}, u32[]{:S(2)}) collective-permute-start(f32[8,128,64]{2,1,0:T(8,128)} %multiply_add_fusion.2), channel_id=1, source_target_pairs={{0,8},{8,16},{16,24},{24,32},{32,40},{40,48},{48,56},{56,64},{64,7... | collective-permute-start | bytes 786440 | tf_op jit(solution)/shard_map/while/body/eval_jaxpr/ppermute | solution.py:12
  542.5 15.6 %collective-permute-start = (f32[8,128,64]{2,1,0:T(8,128)}, f32[8,128,64]{2,1,0:T(8,128)S(1)}, u32[]{:S(2)}, u32[]{:S(2)}) collective-permute-start(f32[8,128,64]{2,1,0:T(8,128)} %multiply_add_fusion.2), channel_id=1, source_target_pairs={{0,8},{8,16},{16,24},{24,32},{32,40},{40,48},{48,56},{56,64},{64,7... | collective-permute-start | bytes 786440 | tf_op jit(solution)/shard_map/while/body/eval_jaxpr/ppermute | solution.py:12
  559.1 17.7 %collective-permute-start = (f32[8,128,64]{2,1,0:T(8,128)}, f32[8,128,64]{2,1,0:T(8,128)S(1)}, u32[]{:S(2)}, u32[]{:S(2)}) collective-permute-start(f32[8,128,64]{2,1,0:T(8,128)} %multiply_add_fusion.2), channel_id=1, source_target_pairs={{0,8},{8,16},{16,24},{24,32},{32,40},{40,48},{48,56},{56,64},{64,7... | collective-permute-start | bytes 786440 | tf_op jit(solution)/shard_map/while/body/eval_jaxpr/ppermute | solution.py:12
  577.7 19.4 %collective-permute-start = (f32[8,128,64]{2,1,0:T(8,128)}, f32[8,128,64]{2,1,0:T(8,128)S(1)}, u32[]{:S(2)}, u32[]{:S(2)}) collective-permute-start(f32[8,128,64]{2,1,0:T(8,128)} %multiply_add_fusion.2), channel_id=1, source_target_pairs={{0,8},{8,16},{16,24},{24,32},{32,40},{40,48},{48,56},{56,64},{64,7... | collective-permute-start | bytes 786440 | tf_op jit(solution)/shard_map/while/body/eval_jaxpr/ppermute | solution.py:12
  598.0 18.8 %collective-permute-start = (f32[8,128,64]{2,1,0:T(8,128)}, f32[8,128,64]{2,1,0:T(8,128)S(1)}, u32[]{:S(2)}, u32[]{:S(2)}) collective-permute-start(f32[8,128,64]{2,1,0:T(8,128)} %multiply_add_fusion.2), channel_id=1, source_target_pairs={{0,8},{8,16},{16,24},{24,32},{32,40},{40,48},{48,56},{56,64},{64,7... | collective-permute-start | bytes 786440 | tf_op jit(solution)/shard_map/while/body/eval_jaxpr/ppermute | solution.py:12
  617.7 16.6 %collective-permute-start = (f32[8,128,64]{2,1,0:T(8,128)}, f32[8,128,64]{2,1,0:T(8,128)S(1)}, u32[]{:S(2)}, u32[]{:S(2)}) collective-permute-start(f32[8,128,64]{2,1,0:T(8,128)} %multiply_add_fusion.2), channel_id=1, source_target_pairs={{0,8},{8,16},{16,24},{24,32},{32,40},{40,48},{48,56},{56,64},{64,7... | collective-permute-start | bytes 786440 | tf_op jit(solution)/shard_map/while/body/eval_jaxpr/ppermute | solution.py:12
  635.3 14.9 %collective-permute-start = (f32[8,128,64]{2,1,0:T(8,128)}, f32[8,128,64]{2,1,0:T(8,128)S(1)}, u32[]{:S(2)}, u32[]{:S(2)}) collective-permute-start(f32[8,128,64]{2,1,0:T(8,128)} %multiply_add_fusion.2), channel_id=1, source_target_pairs={{0,8},{8,16},{16,24},{24,32},{32,40},{40,48},{48,56},{56,64},{64,7... | collective-permute-start | bytes 786440 | tf_op jit(solution)/shard_map/while/body/eval_jaxpr/ppermute | solution.py:12
  651.1 12.9 %collective-permute-start = (f32[8,128,64]{2,1,0:T(8,128)}, f32[8,128,64]{2,1,0:T(8,128)S(1)}, u32[]{:S(2)}, u32[]{:S(2)}) collective-permute-start(f32[8,128,64]{2,1,0:T(8,128)} %multiply_add_fusion.2), channel_id=1, source_target_pairs={{0,8},{8,16},{16,24},{24,32},{32,40},{40,48},{48,56},{56,64},{64,7... | collective-permute-start | bytes 786440 | tf_op jit(solution)/shard_map/while/body/eval_jaxpr/ppermute | solution.py:12
  664.9 10.8 %collective-permute-start = (f32[8,128,64]{2,1,0:T(8,128)}, f32[8,128,64]{2,1,0:T(8,128)S(1)}, u32[]{:S(2)}, u32[]{:S(2)}) collective-permute-start(f32[8,128,64]{2,1,0:T(8,128)} %multiply_add_fusion.2), channel_id=1, source_target_pairs={{0,8},{8,16},{16,24},{24,32},{32,40},{40,48},{48,56},{56,64},{64,7... | collective-permute-start | bytes 786440 | tf_op jit(solution)/shard_map/while/body/eval_jaxpr/ppermute | solution.py:12
  676.6 11.6 %collective-permute-start = (f32[8,128,64]{2,1,0:T(8,128)}, f32[8,128,64]{2,1,0:T(8,128)S(1)}, u32[]{:S(2)}, u32[]{:S(2)}) collective-permute-start(f32[8,128,64]{2,1,0:T(8,128)} %multiply_add_fusion.2), channel_id=1, source_target_pairs={{0,8},{8,16},{16,24},{24,32},{32,40},{40,48},{48,56},{56,64},{64,7... | collective-permute-start | bytes 786440 | tf_op jit(solution)/shard_map/while/body/eval_jaxpr/ppermute | solution.py:12
  689.1 11.4 %collective-permute-start = (f32[8,128,64]{2,1,0:T(8,128)}, f32[8,128,64]{2,1,0:T(8,128)S(1)}, u32[]{:S(2)}, u32[]{:S(2)}) collective-permute-start(f32[8,128,64]{2,1,0:T(8,128)} %multiply_add_fusion.2), channel_id=1, source_target_pairs={{0,8},{8,16},{16,24},{24,32},{32,40},{40,48},{48,56},{56,64},{64,7... | collective-permute-start | bytes 786440 | tf_op jit(solution)/shard_map/while/body/eval_jaxpr/ppermute | solution.py:12
  715.7 2.1 copy-start.6
  715.7 2.1 copy-start.7
  717.4 1.2 copy-start.2
  717.4 1.5 copy-start.5
  726.7 4.8 copy-start.9
  726.7 4.8 copy-start.11
  726.7 4.8 copy-start.13
  731.5 54.0 %copy-start.12 = (f32[512]{0:T(512)S(1)}, f32[512]{0:T(512)}, u32[]{:S(2)}) copy-start(f32[512]{0:T(512)} %param.28) | copy-start | bytes 6148
  793.3 0.7 copy-start.17
  793.3 0.7 copy-start.18
  793.3 0.8 copy-start.20
Sparse Core Ops, SparseCore 0:
  9.9 75.0 all-gather.9
  86.8 41.0 all-gather.5
  130.5 78.7 all-gather.7
  211.7 75.2 all-gather.11
  793.5 73.4 reduce-scatter.1
where the time goes:
time: 878 us; the launch traced here: 876 us
  waiting for transfers between devices  483 us (55%)
  starting transfers between devices  162 us (18%)
  blocking collectives  90.2 us (10%)
  other arithmetic  68 us (8%)
  local copies, waits for them, and re-layouts  29.4 us (3%)
  matrix products  28.5 us (3%)
  between operations  13.5 us (2%)
    ppermute x33, waiting for transfers between devices, passed_along(): return lax.ppermute(value, axis, pairs)  270 us
    ppermute x33, starting transfers between devices, passed_along(): return lax.ppermute(value, axis, pairs)  162 us
    reduce_scatter x1, waiting for transfers between devices, on_device(): lax.psum_scatter(partial_out, 'tp', scatter_dimension=1, tiled=True)  72.8 us
    all_gather x1, waiting for transfers between devices, on_device(): lax.all_gather(w_inner, 'seq', axis=0, tiled=True)  67.3 us
    psum x1, blocking collectives, on_device(): squares = lax.psum(jnp.sum(gated * gated, axis=1), 'tp')  48.3 us
    all_gather x1, waiting for transfers between devices, on_device(): whole = lax.all_gather(tokens, 'tp', axis=1, tiled=True)  42.9 us
    all_gather x1, blocking collectives, on_device(): lax.all_gather(w_step, 'seq', axis=0, tiled=True)  41.9 us
    add x31, other arithmetic, relay(): block_gain[:, None, None] * entering_now + block_state  28.2 us
  transfers between devices with their start and end apart: 38, of which 35 were waited for; matrix products, arithmetic and copies ran while one was open for 13% of the time, Pallas kernels for 0%

commit v1 on v0

--- a/solution.py
+++ b/solution.py
@@ -62,22 +62,17 @@
     in_block = jnp.arange(row_count, dtype=jnp.int32) % BLOCK
     carry_on = jnp.repeat(local_start == 0, BLOCK)
     whole = lax.all_gather(tokens, "tp", axis=1, tiled=True)
-    pieces = (
-        lax.all_gather(w_inner, "seq", axis=0, tiled=True),
-        lax.all_gather(w_states, "seq", axis=0, tiled=True),
-        lax.all_gather(w_step, "seq", axis=0, tiled=True),
+    local_rows = w_inner.shape[0]
+    joined = jnp.concatenate(
+        [w_inner.reshape(local_rows, 2 * inner_here), w_states, w_step], axis=1
     )
-    count = pieces[0].shape[0]
-    inner_sum = jnp.dot(
-        whole, pieces[0].reshape(count, 2 * inner_here), preferred_element_type=jnp.float32
-    )
-    states_sum = jnp.dot(whole, pieces[1], preferred_element_type=jnp.float32)
-    step_sum = jnp.dot(whole, pieces[2], preferred_element_type=jnp.float32)
-    projected = inner_sum.astype(jnp.bfloat16)
+    weights = lax.all_gather(joined, "seq", axis=0, tiled=True)
+    all_sum = jnp.dot(whole, weights, preferred_element_type=jnp.float32)
+    projected = all_sum.astype(jnp.bfloat16)
     gate_in = projected[:, :inner_here]
-    x_in = projected[:, inner_here:]
-    bc_in = states_sum.astype(jnp.bfloat16)
-    step_raw = step_sum.astype(jnp.bfloat16)
+    x_in = projected[:, inner_here : 2 * inner_here]
+    bc_in = projected[:, 2 * inner_here : 2 * inner_here + 2 * state_size]
+    step_raw = projected[:, 2 * inner_here + 2 * state_size :]
     edge_inner, edge_states = passed_along(
         (x_in[row_count - lag_rows :], bc_in[row_count - lag_rows :]), "seq", 1
     )
@@ -117,10 +112,24 @@
         fold_block, (unit_gain, zero_state), (block_gain_each, fresh)
     )
 
-    def relay(iteration, entering_now):
-        return passed_along(block_gain[:, None, None] * entering_now + block_state, "seq", 1)
+    def packed(gain, state):
+        rows = jnp.broadcast_to(gain[:, None, None], (heads_here, 1, head_size))
+        return jnp.concatenate([state, rows], axis=1)
 
-    entering = lax.fori_loop(0, lax.axis_size("seq") - 1, relay, zero_state)
+    prefix = passed_along(packed(block_gain, block_state), "seq", 1)
+    reach = 1
+    while reach < lax.axis_size("seq") - 1:
+        earlier = passed_along(prefix, "seq", reach)
+        gain_now = prefix[:, state_size:, :1]
+        prefix = jnp.concatenate(
+            [
+                gain_now * earlier[:, :state_size] + prefix[:, :state_size],
+                gain_now * earlier[:, state_size:],
+            ],
+            axis=1,
+        )
+        reach *= 2
+    entering = prefix[:, :state_size]
 
     def pass_block(previous, item):
         log_now, keep_now, fresh_now = item

time: 878 us -> 413 us (0.47)
  waiting for transfers between devices: 483 us -> 242 us
  starting transfers between devices: 162 us -> 43.9 us
  blocking collectives: 90.2 us -> 15 us
  other arithmetic: 68 us -> 39.1 us
    ppermute x33 -> x8, waiting for transfers between devices: 270 us -> 64.6 us  [passed_along(): return lax.ppermute(value, axis, pairs)]
    ppermute x33 -> x8, starting transfers between devices: 162 us -> 43.7 us  [passed_along(): return lax.ppermute(value, axis, pairs)]
    all_gather x1 -> x0, blocking collectives: 41.9 us -> none  [on_device(): lax.all_gather(w_step, 'seq', axis=0, tiled=True)]
    psum x1, blocking collectives: 48.3 us -> 15 us  [on_device(): squares = lax.psum(jnp.sum(gated * gated, axis=1), 'tp')]
    add x31 -> x5, other arithmetic: 28.2 us -> 1.44 us  [on_device(): gain_now * earlier[:, :state_size] + prefix[:, :state_size]]
    reduce_scatter x1, waiting for transfers between devices: 72.8 us -> 51.1 us  [on_device(): lax.psum_scatter(partial_out, 'tp', scatter_dimension=1, tiled=True)]
    all_gather x2 -> x1, waiting for transfers between devices: 94.8 us -> 88 us  [on_device(): weights = lax.all_gather(joined, 'seq', axis=0, tiled=True)]
  transfers between devices with their start and end apart: 38 -> 12, of which waited for: 35 -> 9; matrix products, arithmetic and copies ran while one was open for 13% -> 14% of each run, Pallas kernels for 0% -> 0%
where the time goes in v1:
time: 413 us; the launch traced here: 412 us
  waiting for transfers between devices  242 us (59%)
  starting transfers between devices  43.9 us (11%)
  other arithmetic  39.1 us (9%)
  local copies, waits for them, and re-layouts  30.4 us (7%)
  matrix products  27.8 us (7%)
  blocking collectives  15 us (4%)
  between operations  13.7 us (3%)
    all_gather x1, waiting for transfers between devices, on_device(): weights = lax.all_gather(joined, 'seq', axis=0, tiled=True)  88 us
    ppermute x8, waiting for transfers between devices, passed_along(): return lax.ppermute(value, axis, pairs)  64.6 us
    reduce_scatter x1, waiting for transfers between devices, on_device(): lax.psum_scatter(partial_out, 'tp', scatter_dimension=1, tiled=True)  51.1 us
    ppermute x8, starting transfers between devices, passed_along(): return lax.ppermute(value, axis, pairs)  43.7 us
    all_gather x1, waiting for transfers between devices, on_device(): whole = lax.all_gather(tokens, 'tp', axis=1, tiled=True)  37.3 us
    psum x1, blocking collectives, on_device(): squares = lax.psum(jnp.sum(gated * gated, axis=1), 'tp')  15 us
    dot_general x1, matrix products, on_device(): all_sum = jnp.dot(whole, weights, preferred_element_type=jnp.float32)  9.64 us
  transfers between devices with their start and end apart: 12, of which 9 were waited for; matrix products, arithmetic and copies ran while one was open for 14% of the time, Pallas kernels for 0%

profile of v1, /device:TPU:1, one launch (start us, length us, event | category | flops | bytes accessed | tf_op | source)
XLA Modules:
  0.0 411.8 jit_solution(11230645750656030587)
XLA Ops:
  7.3 0.9 copy.99
  9.0 1.4 pad_maximum_fusion.5
  10.6 0.9 select_reduce_fusion
  12.4 0.8 fusion.63
  13.3 0.9 fusion.62
  14.2 37.3 %all-gather.6.cloned.1.call-done = bf16[1024,2048]{1,0:T(8,128)(2,1)} async-done(((bf16[1024,256]{1,0:T(8,128)(2,1)}), bf16[1024,2048]{1,0:T(8,128)(2,1)}) %all-gather.6.cloned.1.call-update) | async-done | bytes 4194320 | tf_op jit(solution)/shard_map/all_gather | solution.py:64
  51.5 88.0 %all-gather.4.cloned.1.call-done = bf16[2048,1288]{1,0:T(8,128)(2,1)} async-done(((bf16[64,1288]{1,0:T(8,128)(2,1)}), bf16[2048,1288]{1,0:T(8,128)(2,1)}) %all-gather.4.cloned.1.call-update) | async-done | bytes 5275664 | tf_op jit(solution)/shard_map/all_gather | solution.py:69
  139.4 9.6 %fusion.10 = bf16[1024,1288]{0,1:T(8,128)(2,1)S(1)} fusion(bf16[2048,1288]{1,0:T(8,128)(2,1)} %all-gather.4.cloned.1.call-done, bf16[1024,2048]{1,0:T(8,128)(2,1)} %all-gather.6.cloned.1.call-done), kind=kOutput, calls=%fused_computation.20 | convolution fusion | flops 5403582464 | bytes 12107776 | tf_op jit(solution)/shard_map/dot_general | solution.py:70
  149.3 1.3 collective-permute-start
  150.7 3.2 collective-permute-start.1
  154.0 2.3 reduce-window.6
  157.5 2.3 slice.171
  160.0 1.2 multiply_convert_fusion.9
  162.1 1.0 copy.83
  163.1 1.8 maximum_convert_fusion
  165.0 3.1 multiply_convert_fusion.5
  168.0 2.7 reshape.136
  170.7 4.9 %fusion.15 = f32[4,8,128,64]{3,2,1,0:T(8,128)} fusion(f32[4,256,128]{2,1,0:T(8,128)} %copy.83, f32[4,256,8]{1,2,0:T(8,128)S(1)} %exponential_multiply_fusion, bf16[4,256,8,64]{1,0,3,2:T(4,128)(2,1)} %reshape.136), kind=kOutput, calls=%fused_computation.27 | convolution fusion | flops 136314880 | bytes 2654208 | tf_op jit(solution)/shard_map/cjhn,cjhp->chnp/dot_general | solution.py:101
  175.6 4.8 %while.26 = (s32[]{:T(128)}, f32[8]{0:T(128)S(1)}, f32[8,128,64]{2,1,0:T(8,128)S(1)}, f32[4,8]{1,0:T(4,128)S(1)}, f32[4,8,128,64]{3,2,1,0:T(8,128)}, /*index=5*/s32[]{:T(128)}, s32[]{:T(128)}) while((s32[]{:T(128)}, f32[8]{0:T(128)S(1)}, f32[8,128,64]{2,1,0:T(8,128)S(1)}, f32[4,8]{1,0:T(4,128)S(1)}, f32[4,8,128,64]{3,2,1,0:T(8,128)}, ...), condition=%wide.region_5.6_spmd.clone, body=%wide.region_4.5_spmd.clone.sunk | while | flops 196627 | bytes 786688 | solution.py:111
  175.6 1.2 bitcast_add_fusion.6
  176.8 1.2 bitcast_add_fusion.6
  178.0 1.2 bitcast_add_fusion.6
  179.2 1.2 bitcast_add_fusion.6
  180.7 4.3 %collective-permute-start.2 = (f32[8,129,64]{1,2,0:T(8,128)S(1)}, f32[8,129,64]{1,2,0:T(8,128)S(1)}, u32[]{:S(2)}, u32[]{:S(2)}) collective-permute-start(f32[8,129,64]{1,2,0:T(8,128)S(1)} %pad_maximum_fusion), channel_id=1, source_target_pairs={{0,8},{8,16},{16,24},{24,32},{32,40},{40,48},{48,56},{56,64},{64,7... | collective-permute-start | bytes 792584 | tf_op jit(solution)/shard_map/ppermute | solution.py:12
  185.0 8.6 %collective-permute-done.2 = f32[8,129,64]{1,2,0:T(8,128)S(1)} collective-permute-done((f32[8,129,64]{1,2,0:T(8,128)S(1)}, f32[8,129,64]{1,2,0:T(8,128)S(1)}, u32[]{:S(2)}, u32[]{:S(2)}) %collective-permute-start.2) | collective-permute-done | bytes 264224 | tf_op jit(solution)/shard_map/ppermute | solution.py:12
  193.6 4.1 %collective-permute-start.3 = (f32[8,129,64]{1,2,0:T(8,128)S(1)}, f32[8,129,64]{1,2,0:T(8,128)S(1)}, u32[]{:S(2)}, u32[]{:S(2)}) collective-permute-start(f32[8,129,64]{1,2,0:T(8,128)S(1)} %collective-permute-done.2), channel_id=1, source_target_pairs={{0,8},{8,16},{16,24},{24,32},{32,40},{40,48},{48,56},{56,64},{64,7... | collective-permute-start | bytes 792584 | tf_op jit(solution)/shard_map/ppermute | solution.py:12
  197.9 7.6 %collective-permute-done.3 = f32[8,129,64]{1,2,0:T(8,128)S(1)} collective-permute-done((f32[8,129,64]{1,2,0:T(8,128)S(1)}, f32[8,129,64]{1,2,0:T(8,128)S(1)}, u32[]{:S(2)}, u32[]{:S(2)}) %collective-permute-start.3) | collective-permute-done | bytes 264224 | tf_op jit(solution)/shard_map/ppermute | solution.py:12
  205.8 3.7 collective-permute-start.4
  209.7 15.5 %collective-permute-done.4 = f32[8,129,64]{1,2,0:T(8,128)S(1)} collective-permute-done((f32[8,129,64]{1,2,0:T(8,128)S(1)}, f32[8,129,64]{1,2,0:T(8,128)S(1)}, u32[]{:S(2)}, u32[]{:S(2)}) %collective-permute-start.4) | collective-permute-done | bytes 264224 | tf_op jit(solution)/shard_map/ppermute | solution.py:12
  225.4 13.6 %collective-permute-start.5 = (f32[8,129,64]{1,2,0:T(8,128)S(1)}, f32[8,129,64]{1,2,0:T(8,128)S(1)}, u32[]{:S(2)}, u32[]{:S(2)}) collective-permute-start(f32[8,129,64]{1,2,0:T(8,128)S(1)} %pad_maximum_fusion.2), channel_id=1, source_target_pairs={{0,32},{8,40},{16,48},{24,56},{32,64},{40,72},{48,80},{56,88},{64,... | collective-permute-start | bytes 792584 | tf_op jit(solution)/shard_map/ppermute | solution.py:12
  239.2 19.2 %collective-permute-done.5 = f32[8,129,64]{1,2,0:T(8,128)S(1)} collective-permute-done((f32[8,129,64]{1,2,0:T(8,128)S(1)}, f32[8,129,64]{1,2,0:T(8,128)S(1)}, u32[]{:S(2)}, u32[]{:S(2)}) %collective-permute-start.5) | collective-permute-done | bytes 264224 | tf_op jit(solution)/shard_map/ppermute | solution.py:12
  260.0 8.6 %collective-permute-start.6 = (f32[8,129,64]{1,2,0:T(8,128)}, f32[8,129,64]{1,2,0:T(8,128)}, u32[]{:S(2)}, u32[]{:S(2)}) collective-permute-start(f32[8,129,64]{1,2,0:T(8,128)} %pad_maximum_fusion.3), channel_id=1, source_target_pairs={{0,64},{8,72},{16,80},{24,88},{32,96},{40,104},{48,112},{56,120},{... | collective-permute-start | bytes 792584 | tf_op jit(solution)/shard_map/ppermute | solution.py:12
  269.4 1.1 copy.96
  270.6 0.9 slice_reduce_fusion.2
  271.5 6.0 %collective-permute-done.6 = f32[8,129,64]{1,2,0:T(8,128)} collective-permute-done((f32[8,129,64]{1,2,0:T(8,128)}, f32[8,129,64]{1,2,0:T(8,128)}, u32[]{:S(2)}, u32[]{:S(2)}) %collective-permute-start.6) | collective-permute-done | bytes 264224 | tf_op jit(solution)/shard_map/ppermute | solution.py:12
  277.5 1.0 slice_multiply_fusion.2
  278.6 1.0 fusion.41
  279.7 4.9 %collective-permute-start.7 = (f32[8,129,64]{1,2,0:T(8,128)S(1)}, f32[8,129,64]{1,2,0:T(8,128)S(1)}, u32[]{:S(2)}, u32[]{:S(2)}) collective-permute-start(f32[8,129,64]{1,2,0:T(8,128)S(1)} %pad_maximum_fusion.4), channel_id=1, source_target_pairs={{0,128},{8,136},{16,144},{24,152},{32,160},{40,168},{48,176},{56,1... | collective-permute-start | bytes 792584 | tf_op jit(solution)/shard_map/ppermute | solution.py:12
  284.6 1.3 fusion.37
  286.0 7.6 %collective-permute-done.7 = f32[8,129,64]{1,2,0:T(8,128)S(1)} collective-permute-done((f32[8,129,64]{1,2,0:T(8,128)S(1)}, f32[8,129,64]{1,2,0:T(8,128)S(1)}, u32[]{:S(2)}, u32[]{:S(2)}) %collective-permute-start.7) | collective-permute-done | bytes 264224 | tf_op jit(solution)/shard_map/ppermute | solution.py:12
  294.0 20.6 %while.25 = (s32[]{:T(128)}, f32[8,128,64]{2,1,0:T(8,128)S(1)}, bf16[4,8,128,64]{3,2,1,0:T(8,128)(2,1)}, f32[4,8]{1,0:T(4,128)}, f32[4]{0:T(128)}, /*index=5*/f32[4,8,128,64]{3,2,1,0:T(8,128)}, s32[]{:T(128)}) while((s32[]{:T(128)}, f32[8,128,64]{2,1,0:T(8,128)S(1)}, bf16[4,8,128,64]{3,2,1,0:T(8,128)(2,1)}, f32[4,8]{1,0:T(4,128)}, ...), condition=%wide.region_7.8_spmd, body=%wide.region_6.7_spmd.sunk | while | flops 262146 | bytes 1574085 | solution.py:139
  294.0 1.2 dynamic_slice.45
  295.2 1.4 bitcast_dynamic-update-slice_fusion.2
  297.3 1.8 bitcast_add_fusion.5
  299.1 1.2 dynamic_slice.45
  300.4 1.4 bitcast_dynamic-update-slice_fusion.2
  302.5 1.8 bitcast_add_fusion.5
  304.3 1.2 dynamic_slice.45
  305.5 1.4 bitcast_dynamic-update-slice_fusion.2
  307.6 1.8 bitcast_add_fusion.5
  309.4 1.2 dynamic_slice.45
  310.7 1.4 bitcast_dynamic-update-slice_fusion.2
  312.8 1.8 bitcast_add_fusion.5
  314.6 2.4 copy.90
  317.0 1.6 fusion.64
  318.7 2.4 bitcast_add_fusion.2
  321.1 1.4 copy.91
  323.0 1.2 copy-done.2
  324.3 3.7 multiply_reduce_fusion
  328.0 15.0 %psum.7 = f32[1024]{0:T(1024)S(1)} all-reduce(f32[1024]{0:T(1024)S(1)} %get-tuple-element.165), channel_id=1, replica_groups=mesh['seq'=32,'tp'=8] {'tp'}, use_global_device_ids=true, to_apply=%region_9.10 | all-reduce | flops 1024 | bytes 8192 | tf_op jit(solution)/shard_map/psum | solution.py:148
  343.0 7.9 %fusion.25 = f32[1024,2048]{0,1:T(8,128)} fusion(bf16[512,2048]{0,1:T(8,128)(2,1)} %all-gather.8.cloned.1.call-done, f32[1024,512]{0,1:T(8,128)} %get-tuple-element.166, f32[512]{0:T(512)S(1)} %copy-done.17, f32[1024]{0:T(1024)S(1)} %add_rsqrt_fusion), kind=kOutput, calls=%fused_computation.46 | convolution fusion | flops 2149056512 | bytes 12589056 | tf_op jit(solution)/shard_map/dot_general | solution.py:151
  351.9 51.1 %reduce-scatter.2.cloned.1.call-done = f32[1024,256]{0,1:T(8,128)} async-done(((f32[1024,2048]{0,1:T(8,128)}), f32[1024,256]{0,1:T(8,128)}) %reduce-scatter.2.cloned.1.call-update) | async-done | bytes 1048592 | tf_op jit(solution)/shard_map/reduce_scatter | solution.py:156
  402.9 1.3 select_convert_fusion
  404.2 1.0 copy.93
  (126 shorter events, 13.7 us)
Async XLA Ops:
  6.5 44.9 %all-gather.6.cloned.1.call-start = ((), (), s32[]{:S(2)}) async-start(), calls=%async_computation.2 | async-start | bytes 4718592 | tf_op jit(solution)/shard_map/all_gather | solution.py:64
  7.3 132.2 %all-gather.4.cloned.1.call-start = ((), (), s32[]{:S(2)}) async-start(), calls=%async_computation.1 | async-start | bytes 5947392 | tf_op jit(solution)/shard_map/all_gather | solution.py:69
  10.5 332.6 %all-gather.8.cloned.1.call-start = ((), (), s32[]{:S(2)}) async-start(), calls=%async_computation.3 | async-start | bytes 2162688 | tf_op jit(solution)/shard_map/all_gather | solution.py:153
  11.5 137.6 %copy-start.23 = (s32[128]{0:T(128)}, s32[128]{0:T(128)S(1)}, u32[]{:S(2)}) copy-start(s32[128]{0:T(128)S(1)} %select_reduce_fusion) | copy-start | bytes 1540
  12.4 145.0 %copy-start.19 = (f32[4]{0:T(128)}, f32[4]{0:T(128)S(1)}, u32[]{:S(2)}) copy-start(f32[4]{0:T(128)S(1)} %compare_select_fusion.1) | copy-start | bytes 52
  12.4 152.5 %copy-start.8 = (pred[1024]{0:T(1024)(128)(4,1)}, pred[1024]{0:T(1024)(128)(4,1)S(1)}, u32[]{:S(2)}) copy-start(pred[1024]{0:T(1024)(128)(4,1)S(1)} %get-tuple-element.181) | copy-start | bytes 3076
  12.4 152.5 %copy-start.10 = (pred[1024]{0:T(1024)(128)(4,1)}, pred[1024]{0:T(1024)(128)(4,1)S(1)}, u32[]{:S(2)}) copy-start(pred[1024]{0:T(1024)(128)(4,1)S(1)} %get-tuple-element.182) | copy-start | bytes 3076
  12.4 152.5 %copy-start.12 = (pred[1024]{0:T(1024)(128)(4,1)}, pred[1024]{0:T(1024)(128)(4,1)S(1)}, u32[]{:S(2)}) copy-start(pred[1024]{0:T(1024)(128)(4,1)S(1)} %get-tuple-element.183) | copy-start | bytes 3076
  12.4 152.5 %copy-start.14 = (pred[1024]{0:T(1024)(128)(4,1)}, pred[1024]{0:T(1024)(128)(4,1)S(1)}, u32[]{:S(2)}) copy-start(pred[1024]{0:T(1024)(128)(4,1)S(1)} %get-tuple-element.184) | copy-start | bytes 3076
  14.1 139.7 %copy-start.20 = (f32[8]{0:T(128)S(1)}, f32[8]{0:T(128)}, u32[]{:S(2)}) copy-start(f32[8]{0:T(128)} %param.24) | copy-start | bytes 100
  149.1 4.8 %copy-start.1 = (bf16[1024,1288]{0,1:T(8,128)(2,1)}, bf16[1024,1288]{0,1:T(8,128)(2,1)S(1)}, u32[]{:S(2)}) copy-start(bf16[1024,1288]{0,1:T(8,128)(2,1)S(1)} %fusion.10) | copy-start | bytes 7913476
  149.3 13.8 %collective-permute-start = (bf16[3,512]{0,1:T(8,128)(2,1)S(1)}, bf16[3,512]{0,1:T(8,128)(2,1)S(1)}, u32[]{:S(2)}, u32[]{:S(2)}) collective-permute-start(bf16[3,512]{0,1:T(8,128)(2,1)S(1)} %slice.170), channel_id=1, source_target_pairs={{0,8},{8,16},{16,24},{24,32},{32,40},{40,48},{48,56},{56,64},{64,7... | collective-permute-start | bytes 9224 | tf_op jit(solution)/shard_map/ppermute | solution.py:12
  150.7 9.1 %collective-permute-start.1 = (bf16[3,256]{0,1:T(8,128)(2,1)S(1)}, bf16[3,256]{0,1:T(8,128)(2,1)S(1)}, u32[]{:S(2)}, u32[]{:S(2)}) collective-permute-start(bf16[3,256]{0,1:T(8,128)(2,1)S(1)} %slice.179), channel_id=1, source_target_pairs={{0,8},{8,16},{16,24},{24,32},{32,40},{40,48},{48,56},{56,64},{64,7... | collective-permute-start | bytes 4616 | tf_op jit(solution)/shard_map/ppermute | solution.py:12
  154.0 5.8 %slice-start = ((bf16[1024,1288]{0,1:T(8,128)(2,1)}), bf16[1024,256]{0,1:T(8,128)(2,1)S(1)}, s32[]{:S(2)}) async-start(bf16[1024,1288]{0,1:T(8,128)(2,1)} %copy-done.1), calls=%async_computation.5 | async-start | bytes 1048576 | tf_op jit(solution)/shard_map/slice | solution.py:74
  157.3 2.7 copy-start.7
  180.7 12.9 %collective-permute-start.2 = (f32[8,129,64]{1,2,0:T(8,128)S(1)}, f32[8,129,64]{1,2,0:T(8,128)S(1)}, u32[]{:S(2)}, u32[]{:S(2)}) collective-permute-start(f32[8,129,64]{1,2,0:T(8,128)S(1)} %pad_maximum_fusion), channel_id=1, source_target_pairs={{0,8},{8,16},{16,24},{24,32},{32,40},{40,48},{48,56},{56,64},{64,7... | collective-permute-start | bytes 792584 | tf_op jit(solution)/shard_map/ppermute | solution.py:12
  193.6 11.9 %collective-permute-start.3 = (f32[8,129,64]{1,2,0:T(8,128)S(1)}, f32[8,129,64]{1,2,0:T(8,128)S(1)}, u32[]{:S(2)}, u32[]{:S(2)}) collective-permute-start(f32[8,129,64]{1,2,0:T(8,128)S(1)} %collective-permute-done.2), channel_id=1, source_target_pairs={{0,8},{8,16},{16,24},{24,32},{32,40},{40,48},{48,56},{56,64},{64,7... | collective-permute-start | bytes 792584 | tf_op jit(solution)/shard_map/ppermute | solution.py:12
  205.8 19.4 %collective-permute-start.4 = (f32[8,129,64]{1,2,0:T(8,128)S(1)}, f32[8,129,64]{1,2,0:T(8,128)S(1)}, u32[]{:S(2)}, u32[]{:S(2)}) collective-permute-start(f32[8,129,64]{1,2,0:T(8,128)S(1)} %pad_maximum_fusion.1), channel_id=1, source_target_pairs={{0,16},{8,24},{16,32},{24,40},{32,48},{40,56},{48,64},{56,72},{64,... | collective-permute-start | bytes 792584 | tf_op jit(solution)/shard_map/ppermute | solution.py:12
  225.2 43.4 %copy-start.18 = (f32[8]{0:T(128)S(1)}, f32[8]{0:T(128)}, u32[]{:S(2)}) copy-start(f32[8]{0:T(128)} %param.25) | copy-start | bytes 100
  225.4 32.9 %collective-permute-start.5 = (f32[8,129,64]{1,2,0:T(8,128)S(1)}, f32[8,129,64]{1,2,0:T(8,128)S(1)}, u32[]{:S(2)}, u32[]{:S(2)}) collective-permute-start(f32[8,129,64]{1,2,0:T(8,128)S(1)} %pad_maximum_fusion.2), channel_id=1, source_target_pairs={{0,32},{8,40},{16,48},{24,56},{32,64},{40,72},{48,80},{56,88},{64,... | collective-permute-start | bytes 792584 | tf_op jit(solution)/shard_map/ppermute | solution.py:12
  258.4 0.7 copy-start.4
  260.0 17.5 %collective-permute-start.6 = (f32[8,129,64]{1,2,0:T(8,128)}, f32[8,129,64]{1,2,0:T(8,128)}, u32[]{:S(2)}, u32[]{:S(2)}) collective-permute-start(f32[8,129,64]{1,2,0:T(8,128)} %pad_maximum_fusion.3), channel_id=1, source_target_pairs={{0,64},{8,72},{16,80},{24,88},{32,96},{40,104},{48,112},{56,120},{... | collective-permute-start | bytes 792584 | tf_op jit(solution)/shard_map/ppermute | solution.py:12
  268.6 134.3 %reduce-scatter.2.cloned.1.call-start = ((), (), s32[]{:S(2)}) async-start(), calls=%async_computation.4 | async-start | bytes 9437184 | tf_op jit(solution)/shard_map/reduce_scatter | solution.py:156
  270.6 23.2 %copy-start.3 = (bf16[1024,128]{1,0:T(8,128)(2,1)}, bf16[1024,128]{1,0:T(8,128)(2,1)S(1)}, u32[]{:S(2)}) copy-start(bf16[1024,128]{1,0:T(8,128)(2,1)S(1)} %copy.96) | copy-start | bytes 786436
  279.7 14.0 %collective-permute-start.7 = (f32[8,129,64]{1,2,0:T(8,128)S(1)}, f32[8,129,64]{1,2,0:T(8,128)S(1)}, u32[]{:S(2)}, u32[]{:S(2)}) collective-permute-start(f32[8,129,64]{1,2,0:T(8,128)S(1)} %pad_maximum_fusion.4), channel_id=1, source_target_pairs={{0,128},{8,136},{16,144},{24,152},{32,160},{40,168},{48,176},{56,1... | collective-permute-start | bytes 792584 | tf_op jit(solution)/shard_map/ppermute | solution.py:12
  314.6 4.1 copy-start
  317.0 1.7 copy-start.5
  317.0 1.7 copy-start.6
  322.5 1.8 copy-start.2
  322.5 1.8 copy-start.9
  322.5 1.7 copy-start.11
  322.5 1.7 copy-start.13
  322.5 1.7 copy-start.15
  322.6 1.7 copy-start.16
  324.3 18.7 %copy-start.17 = (f32[512]{0:T(512)S(1)}, f32[512]{0:T(512)}, u32[]{:S(2)}) copy-start(f32[512]{0:T(512)} %param.26) | copy-start | bytes 6148
  350.9 0.7 copy-start.21
  350.9 0.7 copy-start.22
  350.9 0.8 copy-start.24
Sparse Core Ops, SparseCore 0:
  9.2 42.2 all-gather.5
  54.1 85.3 all-gather.3
  268.7 69.7 all-gather.7
  351.1 51.7 reduce-scatter.1

commit v2 on v1

--- a/solution.py
+++ b/solution.py
@@ -1,9 +1,13 @@
 import jax
 import jax.numpy as jnp
 from jax import lax
+from jax.sharding import Mesh
 from jax.sharding import PartitionSpec as P
 
 BLOCK = 256
+LONGEST = 64
+SEQ = ("sx", "sz")
+SEQ_INNER = 8
 
 
 def passed_along(value, axis, by):
@@ -56,7 +60,7 @@
         jnp.where(block_owner[:, None] == request_ids[None, :], lengths[None, :], 0), axis=1
     )
     valid_rows = jnp.clip(own_length - (block_ids - first_block) * BLOCK, 0, BLOCK)
-    seq_index = lax.axis_index("seq")
+    seq_index = lax.axis_index(SEQ)
     local_start = lax.dynamic_slice_in_dim(starting, seq_index * local_blocks, local_blocks)
     local_valid = lax.dynamic_slice_in_dim(valid_rows, seq_index * local_blocks, local_blocks)
     in_block = jnp.arange(row_count, dtype=jnp.int32) % BLOCK
@@ -66,7 +70,9 @@
     joined = jnp.concatenate(
         [w_inner.reshape(local_rows, 2 * inner_here), w_states, w_step], axis=1
     )
-    weights = lax.all_gather(joined, "seq", axis=0, tiled=True)
+    weights = lax.all_gather(
+        lax.all_gather(joined, "sz", axis=0, tiled=True), "sx", axis=0, tiled=True
+    )
     all_sum = jnp.dot(whole, weights, preferred_element_type=jnp.float32)
     projected = all_sum.astype(jnp.bfloat16)
     gate_in = projected[:, :inner_here]
@@ -74,7 +80,7 @@
     bc_in = projected[:, 2 * inner_here : 2 * inner_here + 2 * state_size]
     step_raw = projected[:, 2 * inner_here + 2 * state_size :]
     edge_inner, edge_states = passed_along(
-        (x_in[row_count - lag_rows :], bc_in[row_count - lag_rows :]), "seq", 1
+        (x_in[row_count - lag_rows :], bc_in[row_count - lag_rows :]), SEQ, 1
     )
     x_conv = convolve(x_in, edge_inner, conv_inner, in_block, carry_on)
     bc_conv = convolve(bc_in, edge_states, conv_states, in_block, carry_on)
@@ -116,10 +122,11 @@
         rows = jnp.broadcast_to(gain[:, None, None], (heads_here, 1, head_size))
         return jnp.concatenate([state, rows], axis=1)
 
-    prefix = passed_along(packed(block_gain, block_state), "seq", 1)
+    prefix = passed_along(packed(block_gain, block_state), SEQ, 1)
+    needed = min(-(-(LONGEST - 1) // local_blocks), lax.axis_size(SEQ) - 1)
     reach = 1
-    while reach < lax.axis_size("seq") - 1:
-        earlier = passed_along(prefix, "seq", reach)
+    while reach < needed:
+        earlier = passed_along(prefix, SEQ, reach)
         gain_now = prefix[:, state_size:, :1]
         prefix = jnp.concatenate(
             [
@@ -150,7 +157,9 @@
     normed = (gated * lax.rsqrt(square_mean + 1e-05)[:, None] * norm_gain).astype(jnp.bfloat16)
     partial_out = jnp.dot(
         normed,
-        lax.all_gather(w_output, "seq", axis=1, tiled=True),
+        lax.all_gather(
+            lax.all_gather(w_output, "sz", axis=1, tiled=True), "sx", axis=1, tiled=True
+        ),
         preferred_element_type=jnp.float32,
     )
     summed = lax.psum_scatter(partial_out, "tp", scatter_dimension=1, tiled=True)
@@ -159,24 +168,28 @@
 
 
 def solution(mesh):
+    seq_count, tp_count = mesh.devices.shape
+    split = Mesh(
+        mesh.devices.reshape(seq_count // SEQ_INNER, SEQ_INNER, tp_count), ("sx", "sz", "tp")
+    )
     return jax.shard_map(
         on_device,
-        mesh=mesh,
+        mesh=split,
         in_specs=(
-            P("seq", "tp"),
-            P("seq", None, "tp"),
-            P("seq", None),
-            P("seq", "tp"),
+            P(SEQ, "tp"),
+            P(SEQ, None, "tp"),
+            P(SEQ, None),
+            P(SEQ, "tp"),
             P(None, "tp"),
             P(),
             P("tp"),
             P("tp"),
             P("tp"),
             P("tp"),
-            P("tp", "seq"),
+            P("tp", SEQ),
             P(),
             P(),
         ),
-        out_specs=P("seq", "tp"),
+        out_specs=P(SEQ, "tp"),
         check_vma=False,
     )

time: 413 us -> 451 us (1.092)
  blocking collectives: 15 us -> 69.7 us
  starting transfers between devices: 43.9 us -> 33.5 us
    all_gather x0 -> x1, blocking collectives: none -> 40.6 us  [on_device(): lax.all_gather(w_output, 'sz', axis=1, tiled=True)]
    ppermute x8 -> x7, waiting for transfers between devices: 64.6 us -> 44.4 us  [passed_along(): return lax.ppermute(value, axis, pairs)]
    all_gather x2 -> x3, waiting for transfers between devices: 88 us -> 104 us  [the longest x1 66 us: on_device(): lax.all_gather(lax.all_gather(joined, 'sz', axis=0, tiled=True), 'sx', ax...]
    psum x1, blocking collectives: 15 us -> 29 us  [on_device(): squares = lax.psum(jnp.sum(gated * gated, axis=1), 'tp')]
    ppermute x8 -> x7, starting transfers between devices: 43.7 us -> 33.3 us  [passed_along(): return lax.ppermute(value, axis, pairs)]
    all_gather x1, waiting for transfers between devices: 37.3 us -> 42.1 us  [on_device(): whole = lax.all_gather(tokens, 'tp', axis=1, tiled=True)]
  transfers between devices with their start and end apart: 12 -> 12, of which waited for: 9 -> 8; matrix products, arithmetic and copies ran while one was open for 14% -> 11% of each run, Pallas kernels for 0% -> 0%
where the time goes in v2:
time: 451 us; the launch traced here: 450 us
  waiting for transfers between devices  238 us (53%)
  blocking collectives  69.7 us (15%)
  other arithmetic  37.5 us (8%)
  starting transfers between devices  33.5 us (7%)
  local copies, waits for them, and re-layouts  28.8 us (6%)
  matrix products  27.8 us (6%)
  between operations  13.8 us (3%)
    all_gather x1, waiting for transfers between devices, on_device(): lax.all_gather(lax.all_gather(joined, 'sz', axis=0, tiled=True), 'sx', ax...  66 us
    reduce_scatter x1, waiting for transfers between devices, on_device(): lax.psum_scatter(partial_out, 'tp', scatter_dimension=1, tiled=True)  47 us
    ppermute x7, waiting for transfers between devices, passed_along(): return lax.ppermute(value, axis, pairs)  44.4 us
    all_gather x1, waiting for transfers between devices, on_device(): whole = lax.all_gather(tokens, 'tp', axis=1, tiled=True)  42.1 us
    all_gather x1, blocking collectives, on_device(): lax.all_gather(w_output, 'sz', axis=1, tiled=True)  40.6 us
    all_gather x1, waiting for transfers between devices, on_device(): lax.all_gather(joined, 'sz', axis=0, tiled=True)  38.2 us
    ppermute x7, starting transfers between devices, passed_along(): return lax.ppermute(value, axis, pairs)  33.3 us
    psum x1, blocking collectives, on_device(): squares = lax.psum(jnp.sum(gated * gated, axis=1), 'tp')  29 us
  transfers between devices with their start and end apart: 12, of which 8 were waited for; matrix products, arithmetic and copies ran while one was open for 11% of the time, Pallas kernels for 0%

profile of v2, /device:TPU:1, one launch (start us, length us, event | category | flops | bytes accessed | tf_op | source)
XLA Modules:
  0.0 449.6 jit_solution(2950230188887680185)
XLA Ops:
  6.6 0.9 copy.99
  7.5 0.8 copy.77
  8.3 1.4 pad_maximum_fusion.4
  10.6 38.2 %all-gather.5.cloned.1.call-done = bf16[512,1288]{1,0:T(8,128)(2,1)} async-done(((bf16[64,1288]{1,0:T(8,128)(2,1)}), bf16[512,1288]{1,0:T(8,128)(2,1)}) %all-gather.5.cloned.1.call-update) | async-done | bytes 1318928 | tf_op jit(solution)/shard_map/all_gather | solution.py:74
  49.8 42.1 %all-gather.9.cloned.1.call-done = bf16[1024,2048]{1,0:T(8,128)(2,1)} async-done(((bf16[1024,256]{1,0:T(8,128)(2,1)}), bf16[1024,2048]{1,0:T(8,128)(2,1)}) %all-gather.9.cloned.1.call-update) | async-done | bytes 4194320 | tf_op jit(solution)/shard_map/all_gather | solution.py:68
  91.9 66.0 %all-gather.7.cloned.1.call-done = bf16[2048,1288]{1,0:T(8,128)(2,1)} async-done(((bf16[512,1288]{1,0:T(8,128)(2,1)}), bf16[2048,1288]{1,0:T(8,128)(2,1)}) %all-gather.7.cloned.1.call-update) | async-done | bytes 5275664 | tf_op jit(solution)/shard_map/all_gather | solution.py:73
  157.9 9.6 %fusion.10 = bf16[1024,1288]{0,1:T(8,128)(2,1)S(1)} fusion(bf16[2048,1288]{1,0:T(8,128)(2,1)} %all-gather.7.cloned.1.call-done, bf16[1024,2048]{1,0:T(8,128)(2,1)} %all-gather.9.cloned.1.call-done), kind=kOutput, calls=%fused_computation.20 | convolution fusion | flops 5403582464 | bytes 12107776 | tf_op jit(solution)/shard_map/dot_general | solution.py:76
  167.8 3.2 collective-permute-start
  171.0 3.2 collective-permute-start.1
  174.3 2.3 reduce-window.6
  176.8 0.7 fusion.59
  177.8 2.3 slice.159
  180.4 1.2 multiply_convert_fusion.9
  181.5 0.7 fusion.60
  182.5 1.0 copy.83
  183.5 1.8 maximum_convert_fusion
  185.3 3.1 multiply_convert_fusion.5
  188.4 2.6 reshape.134
  191.0 4.9 %fusion.15 = f32[4,8,128,64]{3,2,1,0:T(8,128)} fusion(f32[4,256,128]{2,1,0:T(8,128)} %copy.83, f32[4,256,8]{1,2,0:T(8,128)S(1)} %exponential_multiply_fusion, bf16[4,256,8,64]{1,0,3,2:T(4,128)(2,1)} %reshape.134), kind=kOutput, calls=%fused_computation.27 | convolution fusion | flops 136314880 | bytes 2654208 | tf_op jit(solution)/shard_map/cjhn,cjhp->chnp/dot_general | solution.py:107
  195.9 4.8 %while.26 = (s32[]{:T(128)}, f32[8]{0:T(128)S(1)}, f32[8,128,64]{2,1,0:T(8,128)S(1)}, f32[4,8]{1,0:T(4,128)S(1)}, f32[4,8,128,64]{3,2,1,0:T(8,128)}, /*index=5*/s32[]{:T(128)}, s32[]{:T(128)}) while((s32[]{:T(128)}, f32[8]{0:T(128)S(1)}, f32[8,128,64]{2,1,0:T(8,128)S(1)}, f32[4,8]{1,0:T(4,128)S(1)}, f32[4,8,128,64]{3,2,1,0:T(8,128)}, ...), condition=%wide.region_5.6_spmd.clone, body=%wide.region_4.5_spmd.clone.sunk | while | flops 196627 | bytes 786688 | solution.py:117
  196.0 1.2 bitcast_add_fusion.6
  197.2 1.2 bitcast_add_fusion.6
  198.4 1.2 bitcast_add_fusion.6
  199.6 1.2 bitcast_add_fusion.6
  201.1 3.2 collective-permute-start.2
  204.3 9.8 %collective-permute-done.2 = f32[8,129,64]{1,2,0:T(8,128)S(1)} collective-permute-done((f32[8,129,64]{1,2,0:T(8,128)S(1)}, f32[8,129,64]{1,2,0:T(8,128)S(1)}, u32[]{:S(2)}, u32[]{:S(2)}) %collective-permute-start.2) | collective-permute-done | bytes 264224 | tf_op jit(solution)/shard_map/ppermute | solution.py:16
  214.1 4.4 collective-permute-start.3
  218.7 8.8 %collective-permute-done.3 = f32[8,129,64]{1,2,0:T(8,128)S(1)} collective-permute-done((f32[8,129,64]{1,2,0:T(8,128)S(1)}, f32[8,129,64]{1,2,0:T(8,128)S(1)}, u32[]{:S(2)}, u32[]{:S(2)}) %collective-permute-start.3) | collective-permute-done | bytes 264224 | tf_op jit(solution)/shard_map/ppermute | solution.py:16
  227.7 6.1 %collective-permute-start.4 = (f32[8,129,64]{1,2,0:T(8,128)S(1)}, f32[8,129,64]{1,2,0:T(8,128)S(1)}, u32[]{:S(2)}, u32[]{:S(2)}) collective-permute-start(f32[8,129,64]{1,2,0:T(8,128)S(1)} %pad_maximum_fusion.1), channel_id=1, source_target_pairs={{0,16},{8,24},{16,32},{24,40},{32,48},{40,56},{48,64},{56,72},{64,... | collective-permute-start | bytes 792584 | tf_op jit(solution)/shard_map/ppermute | solution.py:16
  234.0 21.2 %collective-permute-done.4 = f32[8,129,64]{1,2,0:T(8,128)S(1)} collective-permute-done((f32[8,129,64]{1,2,0:T(8,128)S(1)}, f32[8,129,64]{1,2,0:T(8,128)S(1)}, u32[]{:S(2)}, u32[]{:S(2)}) %collective-permute-start.4) | collective-permute-done | bytes 264224 | tf_op jit(solution)/shard_map/ppermute | solution.py:16
  256.0 0.8 pad_maximum_fusion.2
  256.8 9.3 %collective-permute-start.5 = (f32[8,129,64]{1,2,0:T(8,128)}, f32[8,129,64]{1,2,0:T(8,128)}, u32[]{:S(2)}, u32[]{:S(2)}) collective-permute-start(f32[8,129,64]{1,2,0:T(8,128)} %pad_maximum_fusion.2), channel_id=1, source_target_pairs={{0,32},{8,40},{16,48},{24,56},{32,64},{40,72},{48,80},{56,88},{64,... | collective-permute-start | bytes 792584 | tf_op jit(solution)/shard_map/ppermute | solution.py:16
  266.1 40.6 %all_gather.18 = bf16[512,512]{0,1:T(8,128)(2,1)} all-gather(bf16[512,64]{0,1:T(8,128)(2,1)S(1)} %copy-done.6), channel_id=1, replica_groups=mesh['sx'=4,'sz'=8,'tp'=8] {'sz'}, dimensions={1}, use_global_device_ids=true | all-gather | bytes 589824 | tf_op jit(solution)/shard_map/all_gather | solution.py:161
  307.6 1.1 copy.96
  308.7 0.9 slice_reduce_fusion.2
  309.7 1.0 slice_multiply_fusion.2
  310.7 1.0 fusion.41
  311.8 4.0 collective-permute-start.6
  315.8 1.3 fusion.37
  317.2 4.5 collective-permute-done.6
  322.0 20.4 %while.25 = (s32[]{:T(128)}, f32[8,128,64]{2,1,0:T(8,128)S(1)}, bf16[4,8,128,64]{3,2,1,0:T(8,128)(2,1)}, f32[4,8]{1,0:T(4,128)}, f32[4]{0:T(128)}, /*index=5*/f32[4,8,128,64]{3,2,1,0:T(8,128)}, s32[]{:T(128)}) while((s32[]{:T(128)}, f32[8,128,64]{2,1,0:T(8,128)S(1)}, bf16[4,8,128,64]{3,2,1,0:T(8,128)(2,1)}, f32[4,8]{1,0:T(4,128)}, ...), condition=%wide.region_7.8_spmd, body=%wide.region_6.7_spmd.sunk | while | flops 262146 | bytes 1574085 | solution.py:146
  322.0 1.2 dynamic_slice.45
  323.2 1.4 bitcast_dynamic-update-slice_fusion.2
  325.3 1.8 bitcast_add_fusion.5
  327.2 1.2 dynamic_slice.45
  328.4 1.4 bitcast_dynamic-update-slice_fusion.2
  330.4 1.8 bitcast_add_fusion.5
  332.3 1.2 dynamic_slice.45
  333.5 1.4 bitcast_dynamic-update-slice_fusion.2
  335.5 1.8 bitcast_add_fusion.5
  337.4 1.2 dynamic_slice.45
  338.6 1.4 bitcast_dynamic-update-slice_fusion.2
  340.7 1.8 bitcast_add_fusion.5
  342.5 2.4 copy.90
  344.9 1.6 fusion.63
  346.6 2.4 bitcast_add_fusion.2
  349.0 1.4 copy.91
  350.9 1.2 copy-done.2
  352.2 3.7 multiply_reduce_fusion
  355.9 29.0 %psum.7 = f32[1024]{0:T(1024)S(1)} all-reduce(f32[1024]{0:T(1024)S(1)} %get-tuple-element.165), channel_id=1, replica_groups=mesh['sx'=4,'sz'=8,'tp'=8] {'tp'}, use_global_device_ids=true, to_apply=%region_9.10 | all-reduce | flops 1024 | bytes 8192 | tf_op jit(solution)/shard_map/psum | solution.py:155
  384.9 7.9 %fusion.25 = f32[1024,2048]{0,1:T(8,128)} fusion(bf16[512,2048]{0,1:T(8,128)(2,1)} %all-gather.11.cloned.1.call-done, f32[1024,512]{0,1:T(8,128)} %get-tuple-element.166, f32[512]{0:T(512)S(1)} %copy-done.20, f32[1024]{0:T(1024)S(1)} %add_rsqrt_fusion), kind=kOutput, calls=%fused_computation.46 | convolution fusion | flops 2149056512 | bytes 12589056 | tf_op jit(solution)/shard_map/dot_general | solution.py:158
  393.8 47.0 %reduce-scatter.2.cloned.1.call-done = f32[1024,256]{0,1:T(8,128)} async-done(((f32[1024,2048]{0,1:T(8,128)}), f32[1024,256]{0,1:T(8,128)}) %reduce-scatter.2.cloned.1.call-update) | async-done | bytes 1048592 | tf_op jit(solution)/shard_map/reduce_scatter | solution.py:165
  440.8 1.3 select_convert_fusion
  442.1 1.0 copy.93
  (134 shorter events, 10.2 us)
Async XLA Ops:
  6.5 42.3 %copy-start.25 = (s32[128]{0:T(128)S(1)}, s32[128]{0:T(128)}, u32[]{:S(2)}) copy-start(s32[128]{0:T(128)} %param.28) | copy-start | bytes 1540
  6.5 43.0 %copy-start.24 = (f32[8]{0:T(128)S(1)}, f32[8]{0:T(128)}, u32[]{:S(2)}) copy-start(f32[8]{0:T(128)} %param.23) | copy-start | bytes 100
  6.5 43.1 %copy-start.19 = (f32[4,256]{1,0:T(4,128)S(1)}, f32[4,256]{1,0:T(4,128)}, u32[]{:S(2)}) copy-start(f32[4,256]{1,0:T(4,128)} %param.22) | copy-start | bytes 12292
  6.5 43.2 %copy-start.18 = (f32[4,512]{1,0:T(4,128)S(1)}, f32[4,512]{1,0:T(4,128)}, u32[]{:S(2)}) copy-start(f32[4,512]{1,0:T(4,128)} %param.21) | copy-start | bytes 24580
  6.5 42.2 %all-gather.5.cloned.1.call-start = ((), (), s32[]{:S(2)}) async-start(), calls=%async_computation.1 | async-start | bytes 1622016 | tf_op jit(solution)/shard_map/all_gather | solution.py:74
  9.8 82.1 %all-gather.9.cloned.1.call-start = ((), (), s32[]{:S(2)}) async-start(), calls=%async_computation.3 | async-start | bytes 4718592 | tf_op jit(solution)/shard_map/all_gather | solution.py:68
  10.5 147.4 %all-gather.7.cloned.1.call-start = ((), (), s32[]{:S(2)}) async-start(), calls=%async_computation.2 | async-start | bytes 7208960 | tf_op jit(solution)/shard_map/all_gather | solution.py:73
  48.8 336.2 %all-gather.11.cloned.1.call-start = ((), (), s32[]{:S(2)}) async-start(), calls=%async_computation.4 | async-start | bytes 2621440 | tf_op jit(solution)/shard_map/all_gather | solution.py:160
  49.0 0.5 copy-start.28
  49.7 128.1 %copy-start.22 = (f32[4]{0:T(128)}, f32[4]{0:T(128)S(1)}, u32[]{:S(2)}) copy-start(f32[4]{0:T(128)S(1)} %compare_select_fusion.1) | copy-start | bytes 52
  49.7 135.6 %copy-start.9 = (pred[1024]{0:T(1024)(128)(4,1)}, pred[1024]{0:T(1024)(128)(4,1)S(1)}, u32[]{:S(2)}) copy-start(pred[1024]{0:T(1024)(128)(4,1)S(1)} %get-tuple-element.181) | copy-start | bytes 3076
  49.7 135.6 %copy-start.11 = (pred[1024]{0:T(1024)(128)(4,1)}, pred[1024]{0:T(1024)(128)(4,1)S(1)}, u32[]{:S(2)}) copy-start(pred[1024]{0:T(1024)(128)(4,1)S(1)} %get-tuple-element.182) | copy-start | bytes 3076
  49.7 135.6 %copy-start.13 = (pred[1024]{0:T(1024)(128)(4,1)}, pred[1024]{0:T(1024)(128)(4,1)S(1)}, u32[]{:S(2)}) copy-start(pred[1024]{0:T(1024)(128)(4,1)S(1)} %get-tuple-element.183) | copy-start | bytes 3076
  49.7 135.6 %copy-start.15 = (pred[1024]{0:T(1024)(128)(4,1)}, pred[1024]{0:T(1024)(128)(4,1)S(1)}, u32[]{:S(2)}) copy-start(pred[1024]{0:T(1024)(128)(4,1)S(1)} %get-tuple-element.184) | copy-start | bytes 3076
  49.8 124.4 %copy-start.23 = (f32[8]{0:T(128)S(1)}, f32[8]{0:T(128)}, u32[]{:S(2)}) copy-start(f32[8]{0:T(128)} %param.24) | copy-start | bytes 100
  167.6 6.6 %copy-start.1 = (bf16[1024,1288]{0,1:T(8,128)(2,1)}, bf16[1024,1288]{0,1:T(8,128)(2,1)S(1)}, u32[]{:S(2)}) copy-start(bf16[1024,1288]{0,1:T(8,128)(2,1)S(1)} %fusion.10) | copy-start | bytes 7913476
  167.8 15.7 %collective-permute-start = (bf16[3,512]{0,1:T(8,128)(2,1)S(1)}, bf16[3,512]{0,1:T(8,128)(2,1)S(1)}, u32[]{:S(2)}, u32[]{:S(2)}) collective-permute-start(bf16[3,512]{0,1:T(8,128)(2,1)S(1)} %slice.158), channel_id=1, source_target_pairs={{0,8},{8,16},{16,24},{24,32},{32,40},{40,48},{48,56},{56,64},{64,7... | collective-permute-start | bytes 9224 | tf_op jit(solution)/shard_map/ppermute | solution.py:16
  171.0 9.1 %collective-permute-start.1 = (bf16[3,256]{0,1:T(8,128)(2,1)S(1)}, bf16[3,256]{0,1:T(8,128)(2,1)S(1)}, u32[]{:S(2)}, u32[]{:S(2)}) collective-permute-start(bf16[3,256]{0,1:T(8,128)(2,1)S(1)} %slice.167), channel_id=1, source_target_pairs={{0,8},{8,16},{16,24},{24,32},{32,40},{40,48},{48,56},{56,64},{64,7... | collective-permute-start | bytes 4616 | tf_op jit(solution)/shard_map/ppermute | solution.py:16
  174.3 5.8 %slice-start = ((bf16[1024,1288]{0,1:T(8,128)(2,1)}), bf16[1024,256]{0,1:T(8,128)(2,1)S(1)}, s32[]{:S(2)}) async-start(bf16[1024,1288]{0,1:T(8,128)(2,1)} %copy-done.1), calls=%async_computation.6 | async-start | bytes 1048576 | tf_op jit(solution)/shard_map/slice | solution.py:80
  177.7 2.7 copy-start.8
  201.1 13.0 %collective-permute-start.2 = (f32[8,129,64]{1,2,0:T(8,128)S(1)}, f32[8,129,64]{1,2,0:T(8,128)S(1)}, u32[]{:S(2)}, u32[]{:S(2)}) collective-permute-start(f32[8,129,64]{1,2,0:T(8,128)S(1)} %pad_maximum_fusion), channel_id=1, source_target_pairs={{0,8},{8,16},{16,24},{24,32},{32,40},{40,48},{48,56},{56,64},{64,7... | collective-permute-start | bytes 792584 | tf_op jit(solution)/shard_map/ppermute | solution.py:16
  214.1 13.4 %collective-permute-start.3 = (f32[8,129,64]{1,2,0:T(8,128)S(1)}, f32[8,129,64]{1,2,0:T(8,128)S(1)}, u32[]{:S(2)}, u32[]{:S(2)}) collective-permute-start(f32[8,129,64]{1,2,0:T(8,128)S(1)} %collective-permute-done.2), channel_id=1, source_target_pairs={{0,8},{8,16},{16,24},{24,32},{32,40},{40,48},{48,56},{56,64},{64,7... | collective-permute-start | bytes 792584 | tf_op jit(solution)/shard_map/ppermute | solution.py:16
  227.6 38.5 %copy-start.6 = (bf16[512,64]{0,1:T(8,128)(2,1)S(1)}, bf16[512,64]{0,1:T(8,128)(2,1)}, u32[]{:S(2)}) copy-start(bf16[512,64]{0,1:T(8,128)(2,1)} %param.27) | copy-start | bytes 196612
  227.7 79.2 %copy-start.21 = (f32[8]{0:T(128)S(1)}, f32[8]{0:T(128)}, u32[]{:S(2)}) copy-start(f32[8]{0:T(128)} %param.25) | copy-start | bytes 100
  227.7 27.5 %collective-permute-start.4 = (f32[8,129,64]{1,2,0:T(8,128)S(1)}, f32[8,129,64]{1,2,0:T(8,128)S(1)}, u32[]{:S(2)}, u32[]{:S(2)}) collective-permute-start(f32[8,129,64]{1,2,0:T(8,128)S(1)} %pad_maximum_fusion.1), channel_id=1, source_target_pairs={{0,16},{8,24},{16,32},{24,40},{32,48},{40,56},{48,64},{56,72},{64,... | collective-permute-start | bytes 792584 | tf_op jit(solution)/shard_map/ppermute | solution.py:16
  255.3 0.7 copy-start.4
  256.8 52.8 %collective-permute-start.5 = (f32[8,129,64]{1,2,0:T(8,128)}, f32[8,129,64]{1,2,0:T(8,128)}, u32[]{:S(2)}, u32[]{:S(2)}) collective-permute-start(f32[8,129,64]{1,2,0:T(8,128)} %pad_maximum_fusion.2), channel_id=1, source_target_pairs={{0,32},{8,40},{16,48},{24,56},{32,64},{40,72},{48,80},{56,88},{64,... | collective-permute-start | bytes 792584 | tf_op jit(solution)/shard_map/ppermute | solution.py:16
  306.8 134.0 %reduce-scatter.2.cloned.1.call-start = ((), (), s32[]{:S(2)}) async-start(), calls=%async_computation.5 | async-start | bytes 9437184 | tf_op jit(solution)/shard_map/reduce_scatter | solution.py:165
  308.7 13.1 %copy-start.3 = (bf16[1024,128]{1,0:T(8,128)(2,1)}, bf16[1024,128]{1,0:T(8,128)(2,1)S(1)}, u32[]{:S(2)}) copy-start(bf16[1024,128]{1,0:T(8,128)(2,1)S(1)} %copy.96) | copy-start | bytes 786436
  311.8 9.9 %collective-permute-start.6 = (f32[8,129,64]{1,2,0:T(8,128)S(1)}, f32[8,129,64]{1,2,0:T(8,128)S(1)}, u32[]{:S(2)}, u32[]{:S(2)}) collective-permute-start(f32[8,129,64]{1,2,0:T(8,128)S(1)} %pad_maximum_fusion.3), channel_id=1, source_target_pairs={{0,64},{8,72},{16,80},{24,88},{32,96},{40,104},{48,112},{56,120},{... | collective-permute-start | bytes 792584 | tf_op jit(solution)/shard_map/ppermute | solution.py:16
  342.5 4.1 copy-start
  344.9 1.7 copy-start.5
  344.9 1.7 copy-start.7
  350.4 1.7 copy-start.2
  350.4 1.7 copy-start.10
  350.4 1.7 copy-start.12
  350.4 1.7 copy-start.14
  350.4 1.7 copy-start.16
  350.4 1.7 copy-start.17
  352.2 32.8 %copy-start.20 = (f32[512]{0:T(512)S(1)}, f32[512]{0:T(512)}, u32[]{:S(2)}) copy-start(f32[512]{0:T(512)} %param.26) | copy-start | bytes 6148
  392.9 0.7 copy-start.26
  392.9 0.7 copy-start.27
  392.9 0.8 copy-start.29
Sparse Core Ops, SparseCore 0:
  9.9 38.8 all-gather.4
  50.6 41.3 all-gather.8
  93.7 64.1 all-gather.6
  306.9 37.4 all-gather.10
  393.0 47.7 reduce-scatter.1

commit v3 on v1

--- a/solution.py
+++ b/solution.py
@@ -4,6 +4,7 @@
 from jax.sharding import PartitionSpec as P
 
 BLOCK = 256
+LONGEST = 64
 
 
 def passed_along(value, axis, by):
@@ -62,17 +63,15 @@
     in_block = jnp.arange(row_count, dtype=jnp.int32) % BLOCK
     carry_on = jnp.repeat(local_start == 0, BLOCK)
     whole = lax.all_gather(tokens, "tp", axis=1, tiled=True)
-    local_rows = w_inner.shape[0]
-    joined = jnp.concatenate(
-        [w_inner.reshape(local_rows, 2 * inner_here), w_states, w_step], axis=1
-    )
-    weights = lax.all_gather(joined, "seq", axis=0, tiled=True)
-    all_sum = jnp.dot(whole, weights, preferred_element_type=jnp.float32)
-    projected = all_sum.astype(jnp.bfloat16)
-    gate_in = projected[:, :inner_here]
-    x_in = projected[:, inner_here : 2 * inner_here]
-    bc_in = projected[:, 2 * inner_here : 2 * inner_here + 2 * state_size]
-    step_raw = projected[:, 2 * inner_here + 2 * state_size :]
+    first_cols = jnp.concatenate([w_inner[:, 1, :], w_states, w_step], axis=1)
+    first_weights = lax.all_gather(first_cols, "seq", axis=0, tiled=True)
+    gate_weights = lax.all_gather(w_inner[:, 0, :], "seq", axis=0, tiled=True)
+    first_sum = jnp.dot(whole, first_weights, preferred_element_type=jnp.float32)
+    projected = first_sum.astype(jnp.bfloat16)
+    x_in = projected[:, :inner_here]
+    bc_in = projected[:, inner_here : inner_here + 2 * state_size]
+    step_raw = projected[:, inner_here + 2 * state_size :]
+    gate_in = jnp.dot(whole, gate_weights, preferred_element_type=jnp.float32).astype(jnp.bfloat16)
     edge_inner, edge_states = passed_along(
         (x_in[row_count - lag_rows :], bc_in[row_count - lag_rows :]), "seq", 1
     )
@@ -102,23 +101,23 @@
     keep_flag = jnp.where(local_start == 1, 0.0, 1.0).astype(jnp.float32)
     block_gain_each = jnp.exp(final_log) * keep_flag[:, None]
 
-    def fold_block(carry, item):
-        gain_now, fresh_now = item
-        return ((carry[0] * gain_now, gain_now[:, None, None] * carry[1] + fresh_now), None)
-
-    zero_state = jnp.zeros((heads_here, state_size, head_size), jnp.float32)
-    unit_gain = jnp.ones((heads_here,), jnp.float32)
-    (block_gain, block_state), _ = lax.scan(
-        fold_block, (unit_gain, zero_state), (block_gain_each, fresh)
-    )
+    block_gain = jnp.ones((heads_here,), jnp.float32)
+    block_state = jnp.zeros((heads_here, state_size, head_size), jnp.float32)
+    gains_in, states_in = [], []
+    for block in range(local_blocks):
+        gains_in.append(block_gain * keep_flag[block])
+        states_in.append(block_state * keep_flag[block])
+        block_gain = block_gain * block_gain_each[block]
+        block_state = block_gain_each[block][:, None, None] * block_state + fresh[block]
 
     def packed(gain, state):
         rows = jnp.broadcast_to(gain[:, None, None], (heads_here, 1, head_size))
         return jnp.concatenate([state, rows], axis=1)
 
     prefix = passed_along(packed(block_gain, block_state), "seq", 1)
+    needed = min(-(-(LONGEST - 1) // local_blocks), lax.axis_size("seq") - 1)
     reach = 1
-    while reach < lax.axis_size("seq") - 1:
+    while reach < needed:
         earlier = passed_along(prefix, "seq", reach)
         gain_now = prefix[:, state_size:, :1]
         prefix = jnp.concatenate(
@@ -130,13 +129,9 @@
         )
         reach *= 2
     entering = prefix[:, :state_size]
-
-    def pass_block(previous, item):
-        log_now, keep_now, fresh_now = item
-        incoming = previous * keep_now
-        return (jnp.exp(log_now)[:, None, None] * incoming + fresh_now, incoming)
-
-    _, incoming_all = lax.scan(pass_block, entering, (final_log, keep_flag, fresh))
+    incoming_all = (
+        jnp.stack(gains_in)[:, :, None, None] * entering[None] + jnp.stack(states_in)
+    )
     incoming_half = incoming_all.astype(jnp.bfloat16)
     y_carry = jnp.exp(cumulative)[:, :, :, None] * jnp.einsum(
         "cin,chnp->cihp", c_rows, incoming_half, preferred_element_type=jnp.float32
@@ -145,17 +140,23 @@
         None, :
     ] * x_conv.astype(jnp.float32)
     gated = y_total * jax.nn.silu(gate_in.astype(jnp.float32))
-    squares = lax.psum(jnp.sum(gated * gated, axis=1), "tp")
-    square_mean = squares / (inner_here * lax.axis_size("tp"))
-    normed = (gated * lax.rsqrt(square_mean + 1e-05)[:, None] * norm_gain).astype(jnp.bfloat16)
+    squares = jnp.sum(gated * gated, axis=1)
+    scaled = (gated * norm_gain).astype(jnp.bfloat16)
     partial_out = jnp.dot(
-        normed,
+        scaled,
         lax.all_gather(w_output, "seq", axis=1, tiled=True),
         preferred_element_type=jnp.float32,
     )
-    summed = lax.psum_scatter(partial_out, "tp", scatter_dimension=1, tiled=True)
+    tp_count = lax.axis_size("tp")
+    cols_here = partial_out.shape[1] // tp_count
+    square_rows = jnp.tile(squares.reshape(row_count // cols_here, cols_here), (1, tp_count))
+    summed = lax.psum_scatter(
+        jnp.concatenate([partial_out, square_rows], axis=0), "tp", scatter_dimension=1, tiled=True
+    )
+    square_mean = summed[row_count:].reshape(row_count) / (inner_here * tp_count)
+    mixed = summed[:row_count] * lax.rsqrt(square_mean + 1e-05)[:, None]
     live = in_block < jnp.repeat(local_valid, BLOCK)
-    return jnp.where(live[:, None], summed, 0.0).astype(jnp.bfloat16)
+    return jnp.where(live[:, None], mixed, 0.0).astype(jnp.bfloat16)
 
 
 def solution(mesh):

time: 413 us -> 384 us (0.930)
  blocking collectives: 15 us -> 0 us
  waiting for transfers between devices: 242 us -> 257 us
  other arithmetic: 39.1 us -> 25.9 us
  local copies, waits for them, and re-layouts: 30.4 us -> 22.1 us
  starting transfers between devices: 43.9 us -> 38.9 us
    psum x1 -> x0, blocking collectives: 15 us -> none  [on_device(): squares = lax.psum(jnp.sum(gated * gated, axis=1), 'tp')]
    all_gather x1 -> x2, waiting for transfers between devices: 88 us -> 74.5 us  [the longest x1 74.5 us: on_device(): first_weights = lax.all_gather(first_cols, 'seq', axis=0, tiled=True)]
    ppermute x8 -> x7, waiting for transfers between devices: 64.6 us -> 77.4 us  [passed_along(): return lax.ppermute(value, axis, pairs)]
    add x8 -> x1, other arithmetic: 11.9 us -> 0.13 us  [on_device(): block_gain_each[block][:, None, None] * block_state + fresh[block]]
    all_gather x1, waiting for transfers between devices: 0.02 us -> 7.9 us  [on_device(): lax.all_gather(w_output, 'seq', axis=1, tiled=True)]
    reshape x2 -> x3, local copies, waits for them, and re-layouts: 1.3 us -> 7.76 us  [the longest x2 7.6 us: on_device(): (y_inner + y_carry).reshape(row_count, inner_here)]
    dynamic_update_slice x4 -> x0, other arithmetic: 5.59 us -> none  [on_device(): lax.scan(pass_block, entering, (final_log, keep_flag, fresh))]
    mul x4, other arithmetic: 0.06 us -> 5.11 us  [the longest x1 2.32 us: on_device(): gains_in.append(block_gain * keep_flag[block])]
where the time goes in v3:
time: 384 us; the launch traced here: 383 us
  waiting for transfers between devices  257 us (67%)
  starting transfers between devices  38.9 us (10%)
  other arithmetic  25.9 us (7%)
  matrix products  24.1 us (6%)
  local copies, waits for them, and re-layouts  22.1 us (6%)
  between operations  14.2 us (4%)
    ppermute x7, waiting for transfers between devices, passed_along(): return lax.ppermute(value, axis, pairs)  77.4 us
    all_gather x1, waiting for transfers between devices, on_device(): first_weights = lax.all_gather(first_cols, 'seq', axis=0, tiled=True)  74.5 us
    reduce_scatter x1, waiting for transfers between devices, on_device(): lax.psum_scatter(jnp.concatenate([partial_out, square_rows], axis=0), 'tp...  55.8 us
    all_gather x1, waiting for transfers between devices, on_device(): whole = lax.all_gather(tokens, 'tp', axis=1, tiled=True)  41.1 us
    ppermute x7, starting transfers between devices, passed_along(): return lax.ppermute(value, axis, pairs)  38.7 us
    all_gather x1, waiting for transfers between devices, on_device(): lax.all_gather(w_output, 'seq', axis=1, tiled=True)  7.9 us
    dot_general x1, matrix products, on_device(): jnp.dot(whole, first_weights, preferred_element_type=jnp.float32)  7.8 us
  transfers between devices with their start and end apart: 12, of which 9 were waited for; matrix products, arithmetic and copies ran while one was open for 14% of the time, Pallas kernels for 0%

profile of v3, /device:TPU:1, one launch (start us, length us, event | category | flops | bytes accessed | tf_op | source)
XLA Modules:
  0.0 382.6 jit_solution(7631663439975435024)
XLA Ops:
  6.5 0.8 copy.88
  7.3 1.2 fusion.70
  8.6 1.4 pad_maximum_fusion.5
  10.0 0.7 all-gather.8.cloned.1.call-update
  10.8 0.6 copy.109
  11.5 0.9 select_reduce_fusion
  12.5 0.5 copy-done.13
  13.2 0.7 neg.19
  13.9 0.6 fusion.73
  14.5 0.8 fusion.72
  15.3 0.9 fusion.71
  16.2 74.5 %all-gather.6.cloned.1.call-done = bf16[2048,776]{1,0:T(8,128)(2,1)} async-done(((bf16[64,776]{1,0:T(8,128)(2,1)}), bf16[2048,776]{1,0:T(8,128)(2,1)}) %all-gather.6.cloned.1.call-update) | async-done | bytes 3178512 | tf_op jit(solution)/shard_map/all_gather | solution.py:67
  90.6 41.1 %all-gather.8.cloned.1.call-done = bf16[1024,2048]{1,0:T(8,128)(2,1)} async-done(((bf16[1024,256]{1,0:T(8,128)(2,1)}), bf16[1024,2048]{1,0:T(8,128)(2,1)}) %all-gather.8.cloned.1.call-update) | async-done | bytes 4194320 | tf_op jit(solution)/shard_map/all_gather | solution.py:65
  131.7 7.8 %convert_bitcast_fusion = bf16[1024,776]{1,0:T(8,128)(2,1)S(1)} fusion(bf16[2048,776]{1,0:T(8,128)(2,1)} %all-gather.6.cloned.1.call-done, bf16[1024,2048]{1,0:T(8,128)(2,1)} %all-gather.8.cloned.1.call-done), kind=kOutput, calls=%fused_computation.36 | convolution fusion | flops 3255574528 | bytes 8962048 | tf_op jit(solution)/shard_map/dot_general | solution.py:69
  139.6 3.2 collective-permute-start.1
  142.7 3.2 collective-permute-start
  145.9 0.3 broadcast_multiply_fusion
  146.3 0.2 copy.91
  146.4 0.2 copy.94
  146.6 2.3 reduce-window.6
  149.2 0.2 slice_reduce_fusion
  149.4 0.6 fusion.66
  150.0 2.3 broadcast_multiply_fusion.3
  152.6 1.4 multiply_convert_fusion.9
  154.0 0.7 fusion.69
  154.8 0.8 convert_element_type.64
  155.6 0.3 maximum_convert_fusion
  156.0 2.2 multiply_convert_fusion.5
  158.2 1.1 reshape.173
  159.3 2.0 copy.95
  161.3 2.8 fusion.11
  164.4 4.0 %collective-permute-start.2 = (f32[8,129,64]{1,2,0:T(8,128)S(1)}, f32[8,129,64]{1,2,0:T(8,128)}, u32[]{:S(2)}, u32[]{:S(2)}) collective-permute-start(f32[8,129,64]{1,2,0:T(8,128)S(1)} %pad_maximum_fusion.1), channel_id=1, source_target_pairs={{0,8},{8,16},{16,24},{24,32},{32,40},{40,48},{48,56},{56,64},{64,7... | collective-permute-start | bytes 792584 | tf_op jit(solution)/shard_map/ppermute | solution.py:13
  168.4 10.1 %collective-permute-done.2 = f32[8,129,64]{1,2,0:T(8,128)} collective-permute-done((f32[8,129,64]{1,2,0:T(8,128)S(1)}, f32[8,129,64]{1,2,0:T(8,128)}, u32[]{:S(2)}, u32[]{:S(2)}) %collective-permute-start.2) | collective-permute-done | bytes 264224 | tf_op jit(solution)/shard_map/ppermute | solution.py:13
  178.5 4.2 %collective-permute-start.3 = (f32[8,129,64]{1,2,0:T(8,128)}, f32[8,129,64]{1,2,0:T(8,128)S(1)}, u32[]{:S(2)}, u32[]{:S(2)}) collective-permute-start(f32[8,129,64]{1,2,0:T(8,128)} %collective-permute-done.2), channel_id=1, source_target_pairs={{0,8},{8,16},{16,24},{24,32},{32,40},{40,48},{48,56},{56,64},{64,7... | collective-permute-start | bytes 792584 | tf_op jit(solution)/shard_map/ppermute | solution.py:13
  183.4 0.6 pad.14.clone
  184.2 0.9 slice_reduce_fusion.4
  185.1 13.7 %collective-permute-done.3 = f32[8,129,64]{1,2,0:T(8,128)S(1)} collective-permute-done((f32[8,129,64]{1,2,0:T(8,128)}, f32[8,129,64]{1,2,0:T(8,128)S(1)}, u32[]{:S(2)}, u32[]{:S(2)}) %collective-permute-start.3) | collective-permute-done | bytes 264224 | tf_op jit(solution)/shard_map/ppermute | solution.py:13
  198.8 0.8 copy-done.3
  199.6 1.0 slice_add_fusion
  200.6 1.1 slice_multiply_fusion.7
  201.8 7.5 %collective-permute-start.4 = (f32[8,129,64]{1,2,0:T(8,128)S(1)}, f32[8,129,64]{1,2,0:T(8,128)S(1)}, u32[]{:S(2)}, u32[]{:S(2)}) collective-permute-start(f32[8,129,64]{1,2,0:T(8,128)S(1)} %pad_maximum_fusion.2), channel_id=1, source_target_pairs={{0,16},{8,24},{16,32},{24,40},{32,48},{40,56},{48,64},{56,72},{64,... | collective-permute-start | bytes 792584 | tf_op jit(solution)/shard_map/ppermute | solution.py:13
  209.6 21.6 %collective-permute-done.4 = f32[8,129,64]{1,2,0:T(8,128)S(1)} collective-permute-done((f32[8,129,64]{1,2,0:T(8,128)S(1)}, f32[8,129,64]{1,2,0:T(8,128)S(1)}, u32[]{:S(2)}, u32[]{:S(2)}) %collective-permute-start.4) | collective-permute-done | bytes 264224 | tf_op jit(solution)/shard_map/ppermute | solution.py:13
  231.4 9.2 %collective-permute-start.5 = (f32[8,129,64]{1,2,0:T(8,128)S(1)}, f32[8,129,64]{1,2,0:T(8,128)S(1)}, u32[]{:S(2)}, u32[]{:S(2)}) collective-permute-start(f32[8,129,64]{1,2,0:T(8,128)S(1)} %pad_maximum_fusion.3), channel_id=1, source_target_pairs={{0,32},{8,40},{16,48},{24,56},{32,64},{40,72},{48,80},{56,88},{64,... | collective-permute-start | bytes 792584 | tf_op jit(solution)/shard_map/ppermute | solution.py:13
  240.6 0.3 fusion.74
  240.9 0.1 slice_reduce_fusion.2
  241.0 23.4 %collective-permute-done.5 = f32[8,129,64]{1,2,0:T(8,128)S(1)} collective-permute-done((f32[8,129,64]{1,2,0:T(8,128)S(1)}, f32[8,129,64]{1,2,0:T(8,128)S(1)}, u32[]{:S(2)}, u32[]{:S(2)}) %collective-permute-start.5) | collective-permute-done | bytes 264224 | tf_op jit(solution)/shard_map/ppermute | solution.py:13
  264.7 7.4 %collective-permute-start.6 = (f32[8,129,64]{1,2,0:T(8,128)S(1)}, f32[8,129,64]{1,2,0:T(8,128)S(1)}, u32[]{:S(2)}, u32[]{:S(2)}) collective-permute-start(f32[8,129,64]{1,2,0:T(8,128)S(1)} %pad_maximum_fusion.4), channel_id=1, source_target_pairs={{0,64},{8,72},{16,80},{24,88},{32,96},{40,104},{48,112},{56,120},{... | collective-permute-start | bytes 792584 | tf_op jit(solution)/shard_map/ppermute | solution.py:13
  272.1 1.9 broadcast_multiply_fusion.1
  274.0 0.1 slice_reduce_fusion.1
  274.2 8.5 %collective-permute-done.6 = f32[8,129,64]{1,2,0:T(8,128)S(1)} collective-permute-done((f32[8,129,64]{1,2,0:T(8,128)S(1)}, f32[8,129,64]{1,2,0:T(8,128)S(1)}, u32[]{:S(2)}, u32[]{:S(2)}) %collective-permute-start.6) | collective-permute-done | bytes 264224 | tf_op jit(solution)/shard_map/ppermute | solution.py:13
  282.8 0.2 fusion.38
  283.0 0.4 fusion.75
  283.4 0.6 copy-done
  284.0 2.4 bitcast_add_fusion
  286.4 2.8 copy.104
  289.2 4.8 %reshape.172 = f32[1024,512]{1,0:T(8,128)} reshape(f32[4,256,8,64]{3,2,1,0:T(8,128)} %copy.104) | data formatting | bytes 4194304 | tf_op jit(solution)/shard_map/reshape | solution.py:139
  294.0 6.4 %multiply_reduce_fusion = (f32[1024]{0:T(1024)S(1)}, f32[1024,512]{1,0:T(8,128)S(1)}) fusion(bf16[1024,2048]{1,0:T(8,128)(2,1)} %all-gather.8.cloned.1.call-done, bf16[2048,1,512]{2,0,1:T(8,128)(2,1)} %all-gather.12.cloned.1.call-done, f32[1024,512]{1,0:T(8,128)} %reshape.172, bf16[1024,512]{1,0:T(8,128)(2,1)S(1)} %multiply_convert_fusion.5, f32[512]{0:T(512)S(1)} %mul.490), kind=kOutput, calls=%fused_computation.31 | convolution fusion | flops 2153774080 | bytes 11540480 | tf_op jit(solution)/shard_map/dot_general | solution.py:74
  300.5 7.9 %all-gather.10.cloned.1.call-done = bf16[512,2048]{0,1:T(8,128)(2,1)} async-done(((bf16[512,64]{0,1:T(8,128)(2,1)}), bf16[512,2048]{0,1:T(8,128)(2,1)}) %all-gather.10.cloned.1.call-update) | async-done | bytes 2097168 | tf_op jit(solution)/shard_map/all_gather | solution.py:147
  308.4 4.0 %fusion.28 = f32[1024,2048]{1,0:T(8,128)S(1)} fusion(bf16[512,2048]{0,1:T(8,128)(2,1)} %all-gather.10.cloned.1.call-done, f32[1024,512]{1,0:T(8,128)S(1)} %get-tuple-element.41, f32[512]{0:T(512)S(1)} %copy-done.4), kind=kOutput, calls=%fused_computation.40 | convolution fusion | flops 2148532224 | bytes 12584960 | tf_op jit(solution)/shard_map/dot_general | solution.py:145
  312.4 3.9 %pad_maximum_fusion = f32[1028,2048]{1,0:T(8,128)} fusion(f32[4,2048]{1,0:T(4,128)S(1)} %bitcast.119, f32[1024,2048]{1,0:T(8,128)S(1)} %fusion.28), kind=kLoop, calls=%fused_computation | loop fusion | flops 2105344 | bytes 16842752 | tf_op jit(solution)/shard_map/concatenate | solution.py:154
  316.3 0.6 copy-done.11
  317.2 55.8 %reduce-scatter.2.cloned.1.call-done = f32[1028,256]{1,0:T(8,128)} async-done(((f32[1028,2048]{1,0:T(8,128)}), f32[1028,256]{1,0:T(8,128)}) %reduce-scatter.2.cloned.1.call-update) | async-done | bytes 1052688 | tf_op jit(solution)/shard_map/reduce_scatter | solution.py:153
  373.0 0.7 fusion.50
  373.7 2.4 fusion.30
  (86 shorter events, 2.8 us)
Async XLA Ops:
  6.5 84.1 %all-gather.6.cloned.1.call-start = ((), (), s32[]{:S(2)}) async-start(), calls=%async_computation.1 | async-start | bytes 3784704 | tf_op jit(solution)/shard_map/all_gather | solution.py:67
  10.0 121.7 %all-gather.8.cloned.1.call-start = ((), (), s32[]{:S(2)}) async-start(), calls=%async_computation.2 | async-start | bytes 4718592 | tf_op jit(solution)/shard_map/all_gather | solution.py:65
  10.7 283.3 %all-gather.12.cloned.1.call-start = ((), (), s32[]{:S(2)}) async-start(), calls=%async_computation.5 | async-start | bytes 2162688 | tf_op jit(solution)/shard_map/all_gather | solution.py:68
  11.5 296.9 %all-gather.10.cloned.1.call-start = ((), (), s32[]{:S(2)}) async-start(), calls=%async_computation.3 | async-start | bytes 2162688 | tf_op jit(solution)/shard_map/all_gather | solution.py:147
  12.4 0.5 copy-start.13
  16.2 129.8 %copy-start.9 = (f32[8]{0:T(128)S(1)}, f32[8]{0:T(128)}, u32[]{:S(2)}) copy-start(f32[8]{0:T(128)} %param.20) | copy-start | bytes 100
  139.5 12.9 %copy-start.1 = (bf16[1024,776]{1,0:T(8,128)(2,1)}, bf16[1024,776]{1,0:T(8,128)(2,1)S(1)}, u32[]{:S(2)}) copy-start(bf16[1024,776]{1,0:T(8,128)(2,1)S(1)} %convert_bitcast_fusion) | copy-start | bytes 4767748
  139.6 12.9 %collective-permute-start.1 = (bf16[3,256]{1,0:T(4,128)(2,1)S(1)}, bf16[3,256]{1,0:T(4,128)(2,1)S(1)}, u32[]{:S(2)}, u32[]{:S(2)}) collective-permute-start(bf16[3,256]{1,0:T(4,128)(2,1)S(1)} %slice.235), channel_id=1, source_target_pairs={{0,8},{8,16},{16,24},{24,32},{32,40},{40,48},{48,56},{56,64},{64,7... | collective-permute-start | bytes 4616 | tf_op jit(solution)/shard_map/ppermute | solution.py:13
  142.7 12.9 %collective-permute-start = (bf16[3,512]{1,0:T(4,128)(2,1)S(1)}, bf16[3,512]{1,0:T(4,128)(2,1)S(1)}, u32[]{:S(2)}, u32[]{:S(2)}) collective-permute-start(bf16[3,512]{1,0:T(4,128)(2,1)S(1)} %slice.226), channel_id=1, source_target_pairs={{0,8},{8,16},{16,24},{24,32},{32,40},{40,48},{48,56},{56,64},{64,7... | collective-permute-start | bytes 9224 | tf_op jit(solution)/shard_map/ppermute | solution.py:13
  154.0 1.6 slice-start
  161.3 3.0 copy-start.5
  164.0 20.0 %copy-start.10 = (f32[8]{0:T(128)S(1)}, f32[8]{0:T(128)}, u32[]{:S(2)}) copy-start(f32[8]{0:T(128)} %param.21) | copy-start | bytes 100
  164.2 45.1 %copy-start.6 = (f32[1,8]{1,0:T(1,128)S(1)}, f32[1,8]{1,0:T(1,128)}, u32[]{:S(2)}) copy-start(f32[1,8]{1,0:T(1,128)} %get-tuple-element.24) | copy-start | bytes 100
  164.2 45.1 %copy-start.7 = (f32[1,8]{1,0:T(1,128)S(1)}, f32[1,8]{1,0:T(1,128)}, u32[]{:S(2)}) copy-start(f32[1,8]{1,0:T(1,128)} %get-tuple-element.28) | copy-start | bytes 100
  164.2 45.1 %copy-start.8 = (f32[1,8]{1,0:T(1,128)S(1)}, f32[1,8]{1,0:T(1,128)}, u32[]{:S(2)}) copy-start(f32[1,8]{1,0:T(1,128)} %get-tuple-element.29) | copy-start | bytes 100
  164.4 14.2 %collective-permute-start.2 = (f32[8,129,64]{1,2,0:T(8,128)S(1)}, f32[8,129,64]{1,2,0:T(8,128)}, u32[]{:S(2)}, u32[]{:S(2)}) collective-permute-start(f32[8,129,64]{1,2,0:T(8,128)S(1)} %pad_maximum_fusion.1), channel_id=1, source_target_pairs={{0,8},{8,16},{16,24},{24,32},{32,40},{40,48},{48,56},{56,64},{64,7... | collective-permute-start | bytes 792584 | tf_op jit(solution)/shard_map/ppermute | solution.py:13
  178.5 20.3 %collective-permute-start.3 = (f32[8,129,64]{1,2,0:T(8,128)}, f32[8,129,64]{1,2,0:T(8,128)S(1)}, u32[]{:S(2)}, u32[]{:S(2)}) collective-permute-start(f32[8,129,64]{1,2,0:T(8,128)} %collective-permute-done.2), channel_id=1, source_target_pairs={{0,8},{8,16},{16,24},{24,32},{32,40},{40,48},{48,56},{56,64},{64,7... | collective-permute-start | bytes 792584 | tf_op jit(solution)/shard_map/ppermute | solution.py:13
  182.8 190.2 %reduce-scatter.2.cloned.1.call-start = ((), (), s32[]{:S(2)}) async-start(), calls=%async_computation.4 | async-start | bytes 9510912 | tf_op jit(solution)/shard_map/reduce_scatter | solution.py:153
  198.8 0.8 copy-start.3
  200.6 39.9 %copy-start.2 = (bf16[1024,128]{1,0:T(8,128)(2,1)S(1)}, bf16[1024,128]{1,0:T(8,128)(2,1)}, u32[]{:S(2)}) copy-start(bf16[1024,128]{1,0:T(8,128)(2,1)} %get-tuple-element.13) | copy-start | bytes 786436
  201.8 29.3 %collective-permute-start.4 = (f32[8,129,64]{1,2,0:T(8,128)S(1)}, f32[8,129,64]{1,2,0:T(8,128)S(1)}, u32[]{:S(2)}, u32[]{:S(2)}) collective-permute-start(f32[8,129,64]{1,2,0:T(8,128)S(1)} %pad_maximum_fusion.2), channel_id=1, source_target_pairs={{0,16},{8,24},{16,32},{24,40},{32,48},{40,56},{48,64},{56,72},{64,... | collective-permute-start | bytes 792584 | tf_op jit(solution)/shard_map/ppermute | solution.py:13
  231.4 33.1 %collective-permute-start.5 = (f32[8,129,64]{1,2,0:T(8,128)S(1)}, f32[8,129,64]{1,2,0:T(8,128)S(1)}, u32[]{:S(2)}, u32[]{:S(2)}) collective-permute-start(f32[8,129,64]{1,2,0:T(8,128)S(1)} %pad_maximum_fusion.3), channel_id=1, source_target_pairs={{0,32},{8,40},{16,48},{24,56},{32,64},{40,72},{48,80},{56,88},{64,... | collective-permute-start | bytes 792584 | tf_op jit(solution)/shard_map/ppermute | solution.py:13
  264.7 18.0 %collective-permute-start.6 = (f32[8,129,64]{1,2,0:T(8,128)S(1)}, f32[8,129,64]{1,2,0:T(8,128)S(1)}, u32[]{:S(2)}, u32[]{:S(2)}) collective-permute-start(f32[8,129,64]{1,2,0:T(8,128)S(1)} %pad_maximum_fusion.4), channel_id=1, source_target_pairs={{0,64},{8,72},{16,80},{24,88},{32,96},{40,104},{48,112},{56,120},{... | collective-permute-start | bytes 792584 | tf_op jit(solution)/shard_map/ppermute | solution.py:13
  282.8 1.2 copy-start
  294.0 14.4 %copy-start.4 = (f32[512]{0:T(512)S(1)}, f32[512]{0:T(512)}, u32[]{:S(2)}) copy-start(f32[512]{0:T(512)} %param.22) | copy-start | bytes 6148
  316.3 0.7 copy-start.11
  316.3 0.7 copy-start.12
  316.3 0.8 copy-start.14
Sparse Core Ops, SparseCore 0:
  10.1 80.4 all-gather.5
  92.5 39.1 all-gather.7
  134.3 75.4 all-gather.11
  212.2 96.1 all-gather.9
  316.4 56.5 reduce-scatter.1
